TPU v7x, 256 devices: a whole 4x4x8 slice. The times are simulated.
256 devices in a mesh: row: 8 (over y, core), col: 32 (over z, x).
Axes of the slice: x: 4, y: 4, z: 8, core: 2. Of those that a mesh axis runs over, the one named last changes fastest.
Arguments:
- prior_solved: bfloat16 [92160, 768], P('col'), may hold values from -6 to 6
- lower_prior: bfloat16 [92160, 2, 3072], P('col', None, 'row'), may hold values from -0.01953125 to 0.01953125
- rhs: bfloat16 [2, 3072, 768], P(None, 'row'), may hold values from -6 to 6
- coupling: bfloat16 [3072, 3072], P('col', 'row'), may hold values from -0.109375 to 0.109375
- inverse_diag: bfloat16 [2, 3072, 3072], P(None, 'col', 'row'), may hold values from -1 to 1, as said below
Outputs:
- solved: bfloat16 [2, 3072, 768], P(None, 'row')
Inputs may be any that keep to these rules, and one draw needn't show every extreme that they name: Each block inverse_diag[b] is the inverse of a unit lower triangular block: entry [b, j, i] is zero for j > i and exactly one for j == i.
All inputs are finite; a program needn't handle non-finite values.
Results may differ from a plain program's by a relative error of at most 0.0056.
Values may be sent and summed in bfloat16 or wider, within the bound.
No kernel may reach another device: no remote copies, remote signals or barrier semaphores. Data moves between devices by JAX's collectives and lax.ppermute only.
A program may use at most 64 MiB of HBM per device.

v0:
```python
import jax
import jax.numpy as jnp
from jax import lax
from jax.sharding import PartitionSpec as P


def in_blocks(array, dim, length):
    dims = array.shape
    blocks = array.reshape(*dims[:dim], length, dims[dim] // length, *dims[dim + 1 :])
    return jnp.moveaxis(blocks, dim, 0)


def sum_at_owner(array, axis, dim):
    length = lax.axis_size(axis)
    blocks = lax.all_to_all(in_blocks(array, dim, length), axis, 0, 0, tiled=True)
    return jnp.sum(blocks, axis=0)


def in_order(blocks, dim):
    blocks = jnp.moveaxis(blocks, 0, dim)
    dims = blocks.shape
    return blocks.reshape(*dims[:dim], dims[dim] * dims[dim + 1], *dims[dim + 2 :])


def sent_to_all(array, axis):
    copies = jnp.broadcast_to(array, (lax.axis_size(axis), *array.shape))
    return lax.all_to_all(copies, axis, split_axis=0, concat_axis=0, tiled=True)


def collect(array, axis, dim):
    return in_order(sent_to_all(array, axis), dim)


def local_product(left_block, right_rows):
    return lax.dot_general(
        left_block, right_rows, (((0,), (0,)), ((), ())), preferred_element_type=jnp.float32
    )


def on_device(prior_solved, lower_prior, rhs, coupling, inverse_diag):
    share_width = rhs.shape[2] // lax.axis_size("col")
    share_start = lax.axis_index("col") * share_width
    stacked = jnp.stack([inverse_diag[0], coupling, inverse_diag[1]])
    whole_blocks = lax.all_gather(stacked, "col", axis=1, tiled=True)
    both_terms = jnp.stack(
        [
            local_product(lower_prior[:, 0, :], prior_solved),
            local_product(lower_prior[:, 1, :], prior_solved),
        ]
    )
    shares = sum_at_owner(both_terms, "col", 2)
    rhs_share = lax.dynamic_slice_in_dim(rhs, share_start, share_width, 2).astype(jnp.float32)

    def apply_share(left_block, vector_rows):
        full_vector = collect(vector_rows, "row", 0)
        return local_product(left_block, full_vector)

    first_reduced = (rhs_share[0] - shares[0]).astype(jnp.bfloat16)
    first_solved = apply_share(whole_blocks[0], first_reduced).astype(jnp.bfloat16)
    cross_term = apply_share(whole_blocks[1], first_solved)
    second_reduced = (rhs_share[1] - shares[1] - cross_term).astype(jnp.bfloat16)
    second_solved = apply_share(whole_blocks[2], second_reduced).astype(jnp.bfloat16)
    solved_share = jnp.stack([first_solved, second_solved])
    return collect(solved_share, "col", 2)


def solution(mesh):
    return jax.shard_map(
        on_device,
        mesh=mesh,
        in_specs=(
            P("col", None),
            P("col", None, "row"),
            P(None, "row", None),
            P("col", "row"),
            P(None, "col", "row"),
        ),
        out_specs=P(None, "row", None),
        check_vma=False,
    )
```

profile of v0, /device:TPU:8, one launch (start us, length us, event | category | flops | bytes accessed | tf_op | source)
XLA Modules:
  0.0 206.5 jit_solution(7152646648683226175)
XLA Ops:
  6.5 0.0 copy-start
  6.5 0.0 all-gather.2.cloned.1.call-start
  6.5 1.0 fusion.22
  7.6 1.6 pad_maximum_fusion
  9.2 0.0 all-gather.2.cloned.1.call-update
  9.2 6.6 %copy.36 = bf16[2880,768]{0,1:T(8,128)(2,1)} copy(bf16[2880,768]{1,0:T(8,128)(2,1)} %param.5) | data formatting | bytes 8847360 | tf_op args[0]
  15.8 9.5 %fusion.21 = (bf16[2880,1,384]{2,1,0:T(2,128)(2,1)S(1)}, bf16[2880,1,384]{2,1,0:T(2,128)(2,1)S(1)}) fusion(bf16[2880,2,384]{2,1,0:T(2,128)(2,1)} %param.6), kind=kLoop, calls=%fused_computation.28 | loop fusion | bytes 8847360 | tf_op jit(solution)/shard_map/slice | solution.py:47
  25.4 0.0 copy-done.1
  25.4 2.6 %fusion.10 = f32[1,384,32,24]{1,2,3,0:T(8,128)S(1)} fusion(bf16[32,24,2880]{2,1,0:T(8,128)(2,1)S(1)} %bitcast.63, bf16[2880,1,384]{2,1,0:T(2,128)(2,1)S(1)} %get-tuple-element.6), kind=kOutput, calls=%fused_computation.14 | convolution fusion | flops 1698693120 | bytes 7815168 | tf_op jit(solution)/shard_map/dot_general | solution.py:35
  27.9 2.6 %fusion.7 = f32[1,384,32,24]{1,2,3,0:T(8,128)S(1)} fusion(bf16[32,24,2880]{2,1,0:T(8,128)(2,1)S(1)} %bitcast.64, bf16[2880,1,384]{2,1,0:T(2,128)(2,1)S(1)} %get-tuple-element.5), kind=kOutput, calls=%fused_computation.13 | convolution fusion | flops 1698693120 | bytes 7815168 | tf_op jit(solution)/shard_map/dot_general | solution.py:35
  30.5 0.2 maximum_bitcast_fusion
  30.7 2.8 %copy.40 = f32[32,2,384,24]{2,3,1,0:T(8,128)} copy(f32[32,2,384,24]{2,0,3,1:T(8,128)S(1)} %maximum_bitcast_fusion) | data formatting | bytes 4718592 | tf_op jit(solution)/shard_map/transpose | solution.py:10
  33.5 11.3 %all-to-all-start = ((f32[32,2,384,24]{2,3,1,0:T(8,128)}), f32[32,2,384,24]{2,3,1,0:T(8,128)S(1)}, u32[]{:S(2)}, u32[]{:S(2)}) async-start(f32[32,2,384,24]{2,3,1,0:T(8,128)} %copy.40), calls=%async_computation | async-start | bytes 4718592 | tf_op jit(solution)/shard_map/all_to_all | solution.py:15
  44.8 0.0 copy-done
  44.8 0.8 constant_dynamic-slice_fusion
  45.7 1.6 copy.46
  47.3 1.4 convert_element_type.18
  48.7 68.0 %all-to-all-done = f32[32,2,384,24]{2,3,1,0:T(8,128)S(1)} async-done(((f32[32,2,384,24]{2,3,1,0:T(8,128)}), f32[32,2,384,24]{2,3,1,0:T(8,128)S(1)}, u32[]{:S(2)}, u32[]{:S(2)}) %all-to-all-start) | async-done | bytes 2359328 | tf_op jit(solution)/shard_map/all_to_all | solution.py:15
  116.7 0.7 reduce_sum.9
  117.4 0.8 fusion.20
  118.2 9.5 %all_to_all.25 = bf16[8,384,24]{1,2,0:T(8,128)(2,1)S(1)} all-to-all(bf16[8,384,24]{1,2,0:T(8,128)(2,1)S(1)} %broadcast_in_dim.12), channel_id=1, replica_groups=mesh['row'=8,'col'=32] {'row'}, dimensions={0} | all-to-all | bytes 294912 | tf_op jit(solution)/shard_map/all_to_all | solution.py:27
  127.7 6.1 %all-gather.2.cloned.1.call-done = bf16[3,3072,384]{2,1,0:T(8,128)(2,1)} async-done(((bf16[3,96,384]{2,1,0:T(8,128)(2,1)}), bf16[3,3072,384]{2,1,0:T(8,128)(2,1)}) %all-gather.2.cloned.1.call-update) | async-done | bytes 7077904 | tf_op jit(solution)/shard_map/all_gather | solution.py:44
  133.8 2.1 %fusion.15 = bf16[384,24]{0,1:T(8,128)(2,1)S(1)} fusion(bf16[3072,24]{0,1:T(8,128)(2,1)S(1)} %bitcast.68, bf16[3,3072,384]{2,1,0:T(8,128)(2,1)} %all-gather.2.cloned.1.call-done), kind=kOutput, calls=%fused_computation.17 | convolution fusion | flops 56632320 | bytes 2525184 | tf_op jit(solution)/shard_map/dot_general | solution.py:35
  136.0 9.5 %all_to_all.26 = bf16[8,384,24]{1,2,0:T(8,128)(2,1)S(1)} all-to-all(bf16[8,384,24]{1,2,0:T(8,128)(2,1)S(1)} %broadcast_in_dim.13), channel_id=1, replica_groups=mesh['row'=8,'col'=32] {'row'}, dimensions={0} | all-to-all | bytes 294912 | tf_op jit(solution)/shard_map/all_to_all | solution.py:27
  145.5 0.0 copy-done.2
  145.6 2.1 %fusion.14 = bf16[384,24]{0,1:T(8,128)(2,1)S(1)} fusion(bf16[3072,24]{0,1:T(8,128)(2,1)S(1)} %bitcast.69, bf16[3,3072,384]{2,1,0:T(8,128)(2,1)} %all-gather.2.cloned.1.call-done, f32[2,384,24]{1,2,0:T(8,128)S(1)} %copy-done.3, f32[2,384,24]{1,2,0:T(8,128)S(1)} %copy-done.2), kind=kOutput, calls=%fused_computation.16 | convolution fusion | flops 56650752 | bytes 2598912 | tf_op jit(solution)/shard_map/dot_general | solution.py:35
  147.7 8.7 %all_to_all.27 = bf16[8,384,24]{1,2,0:T(8,128)(2,1)S(1)} all-to-all(bf16[8,384,24]{1,2,0:T(8,128)(2,1)S(1)} %broadcast_in_dim.14), channel_id=1, replica_groups=mesh['row'=8,'col'=32] {'row'}, dimensions={0} | all-to-all | bytes 294912 | tf_op jit(solution)/shard_map/all_to_all | solution.py:27
  156.4 2.1 %fusion.17 = bf16[1,384,24]{1,2,0:T(8,128)(2,1)S(1)} fusion(bf16[3072,24]{0,1:T(8,128)(2,1)S(1)} %bitcast.70, bf16[3,3072,384]{2,1,0:T(8,128)(2,1)} %all-gather.2.cloned.1.call-done), kind=kOutput, calls=%fused_computation.19 | convolution fusion | flops 56632320 | bytes 2525184 | tf_op jit(solution)/shard_map/dot_general | solution.py:35
  158.5 0.1 broadcast_in_dim.15
  158.6 39.5 %all_to_all.28 = bf16[32,2,384,24]{2,3,1,0:T(8,128)(2,1)S(1)} all-to-all(bf16[32,2,384,24]{2,3,1,0:T(8,128)(2,1)S(1)} %broadcast_in_dim.15), channel_id=1, replica_groups=mesh['row'=8,'col'=32] {'col'}, dimensions={0} | all-to-all | bytes 2359296 | tf_op jit(solution)/shard_map/all_to_all | solution.py:27
  198.1 0.1 copy.44
  198.2 1.5 copy.45
  (11 shorter events, 0.1 us)
Async XLA Ops:
  6.5 38.3 %copy-start = (bf16[2,384,768]{2,1,0:T(8,128)(2,1)S(1)}, bf16[2,384,768]{2,1,0:T(8,128)(2,1)}, u32[]{:S(2)}) copy-start(bf16[2,384,768]{2,1,0:T(8,128)(2,1)} %param.7) | copy-start | bytes 3538948
  6.5 127.3 %all-gather.2.cloned.1.call-start = ((), (), s32[]{:S(2)}) async-start(), calls=%async_computation.5 | async-start | bytes 7299072 | tf_op jit(solution)/shard_map/all_gather | solution.py:44
  15.8 9.5 %copy-start.1 = (bf16[2880,768]{0,1:T(8,128)(2,1)S(1)}, bf16[2880,768]{0,1:T(8,128)(2,1)}, u32[]{:S(2)}) copy-start(bf16[2880,768]{0,1:T(8,128)(2,1)} %copy.36) | copy-start | bytes 13271044
  33.5 83.2 %all-to-all-start = ((f32[32,2,384,24]{2,3,1,0:T(8,128)}), f32[32,2,384,24]{2,3,1,0:T(8,128)S(1)}, u32[]{:S(2)}, u32[]{:S(2)}) async-start(f32[32,2,384,24]{2,3,1,0:T(8,128)} %copy.40), calls=%async_computation | async-start | bytes 4718592 | tf_op jit(solution)/shard_map/all_to_all | solution.py:15
  133.8 11.7 %copy-start.2 = (f32[2,384,24]{1,2,0:T(8,128)S(1)}, f32[2,384,24]{1,2,0:T(8,128)}, u32[]{:S(2)}) copy-start(f32[2,384,24]{1,2,0:T(8,128)} %convert_element_type.18) | copy-start | bytes 221188
  133.8 11.7 %copy-start.3 = (f32[2,384,24]{1,2,0:T(8,128)S(1)}, f32[2,384,24]{1,2,0:T(8,128)}, u32[]{:S(2)}) copy-start(f32[2,384,24]{1,2,0:T(8,128)} %reduce_sum.9) | copy-start | bytes 221188
Sparse Core Ops, SparseCore 0:
  9.9 123.8 all-gather.1
where the time goes:
time: 207 us
  waiting for transfers between devices  74.1 us (36%)
  blocking collectives  67.2 us (32%)
  local copies, waits for them, and re-layouts  24.3 us (12%)
  between operations  13.6 us (7%)
  matrix products  11.4 us (6%)
  starting transfers between devices  11.3 us (5%)
  other arithmetic  4.7 us (2%)
    all_to_all x1, waiting for transfers between devices, sum_at_owner(): lax.all_to_all(in_blocks(array, dim, length), axis, 0, 0, tiled=True)  68 us
    all_to_all x4, blocking collectives, sent_to_all(): return lax.all_to_all(copies, axis, split_axis=0, concat_axis=0, tiled=True)  67.2 us
    dot_general x5, matrix products, local_product(): lax.dot_general(left_block, right_rows, (((0,), (0,)), ((), ())), preferr...  11.4 us
    all_to_all x1, starting transfers between devices, sum_at_owner(): lax.all_to_all(in_blocks(array, dim, length), axis, 0, 0, tiled=True)  11.3 us
    slice x1, local copies, waits for them, and re-layouts, on_device(): lower_prior[:, 0, :]  9.51 us
    unnamed x10, local copies, waits for them, and re-layouts  8.29 us
    all_gather x1, waiting for transfers between devices, on_device(): whole_blocks = lax.all_gather(stacked, 'col', axis=1, tiled=True)  6.11 us
  transfers between devices with their start and end apart: 2, of which 2 were waited for; matrix products, arithmetic and copies ran while one was open for 14% of the time, Pallas kernels for 0%

commit v1 on v0

--- a/solution.py
+++ b/solution.py
@@ -40,28 +40,28 @@
 def on_device(prior_solved, lower_prior, rhs, coupling, inverse_diag):
     share_width = rhs.shape[2] // lax.axis_size("col")
     share_start = lax.axis_index("col") * share_width
-    stacked = jnp.stack([inverse_diag[0], coupling, inverse_diag[1]])
-    whole_blocks = lax.all_gather(stacked, "col", axis=1, tiled=True)
-    both_terms = jnp.stack(
-        [
-            local_product(lower_prior[:, 0, :], prior_solved),
-            local_product(lower_prior[:, 1, :], prior_solved),
-        ]
-    )
-    shares = sum_at_owner(both_terms, "col", 2)
+    depth, blocks, rows = lower_prior.shape
+    both_terms = local_product(lower_prior.reshape(depth, blocks * rows), prior_solved)
+    both_terms = both_terms.reshape(blocks, rows, rhs.shape[2])
+    first_share = sum_at_owner(both_terms[0], "col", 1)
+    second_share = sum_at_owner(both_terms[1], "col", 1)
+    first_block = lax.all_gather(inverse_diag[0], "col", axis=0, tiled=True)
+    cross_block = lax.all_gather(coupling, "col", axis=0, tiled=True)
+    second_block = lax.all_gather(inverse_diag[1], "col", axis=0, tiled=True)
     rhs_share = lax.dynamic_slice_in_dim(rhs, share_start, share_width, 2).astype(jnp.float32)
 
     def apply_share(left_block, vector_rows):
         full_vector = collect(vector_rows, "row", 0)
         return local_product(left_block, full_vector)
 
-    first_reduced = (rhs_share[0] - shares[0]).astype(jnp.bfloat16)
-    first_solved = apply_share(whole_blocks[0], first_reduced).astype(jnp.bfloat16)
-    cross_term = apply_share(whole_blocks[1], first_solved)
-    second_reduced = (rhs_share[1] - shares[1] - cross_term).astype(jnp.bfloat16)
-    second_solved = apply_share(whole_blocks[2], second_reduced).astype(jnp.bfloat16)
-    solved_share = jnp.stack([first_solved, second_solved])
-    return collect(solved_share, "col", 2)
+    first_reduced = (rhs_share[0] - first_share).astype(jnp.bfloat16)
+    first_solved = apply_share(first_block, first_reduced).astype(jnp.bfloat16)
+    first_out = collect(first_solved, "col", 1)
+    cross_term = apply_share(cross_block, first_solved)
+    second_reduced = (rhs_share[1] - second_share - cross_term).astype(jnp.bfloat16)
+    second_solved = apply_share(second_block, second_reduced).astype(jnp.bfloat16)
+    second_out = collect(second_solved, "col", 1)
+    return jnp.stack([first_out, second_out])
 
 
 def solution(mesh):

time: 207 us -> 291 us (1.41)
  waiting for transfers between devices: 74.1 us -> 189 us
  blocking collectives: 67.2 us -> 39.6 us
  starting transfers between devices: 11.3 us -> 27.2 us
  local copies, waits for them, and re-layouts: 24.3 us -> 10.2 us
  other arithmetic: 4.7 us -> 0.3 us
    all_gather x1 -> x3, waiting for transfers between devices: 6.11 us -> 140 us  [the longest x1 60.7 us: on_device(): second_block = lax.all_gather(inverse_diag[1], 'col', axis=0, tiled=True)]
    all_to_all x4 -> x3, blocking collectives: 67.2 us -> 39.6 us  [sent_to_all(): return lax.all_to_all(copies, axis, split_axis=0, concat_axis=0, tiled=True)]
    all_to_all x1 -> x2, waiting for transfers between devices: 68 us -> 43.2 us  [sum_at_owner(): lax.all_to_all(in_blocks(array, dim, length), axis, 0, 0, tiled=True)]
    all_to_all x0 -> x2, starting transfers between devices: none -> 10.4 us  [sent_to_all(): return lax.all_to_all(copies, axis, split_axis=0, concat_axis=0, tiled=True)]
    slice x2, local copies, waits for them, and re-layouts: 10.5 us -> 3.29 us  [the longest x1 1.69 us: on_device(): second_block = lax.all_gather(inverse_diag[1], 'col', axis=0, tiled=True)]
    all_to_all x1 -> x2, starting transfers between devices: 11.3 us -> 16.6 us  [sum_at_owner(): lax.all_to_all(in_blocks(array, dim, length), axis, 0, 0, tiled=True)]
    all_to_all x0 -> x2, waiting for transfers between devices: none -> 4.75 us  [sent_to_all(): return lax.all_to_all(copies, axis, split_axis=0, concat_axis=0, tiled=True)]
    unnamed x10 -> x8, local copies, waits for them, and re-layouts: 8.29 us -> 3.65 us
  transfers between devices with their start and end apart: 2 -> 7, of which waited for: 2 -> 6; matrix products, arithmetic and copies ran while one was open for 14% -> 6% of each run, Pallas kernels for 0% -> 0%
where the time goes in v1:
time: 291 us; the launch traced here: 290 us
  waiting for transfers between devices  189 us (65%)
  blocking collectives  39.6 us (14%)
  starting transfers between devices  27.2 us (9%)
  between operations  13.3 us (5%)
  matrix products  10.5 us (4%)
  local copies, waits for them, and re-layouts  10.2 us (4%)
    all_gather x1, waiting for transfers between devices, on_device(): second_block = lax.all_gather(inverse_diag[1], 'col', axis=0, tiled=True)  60.7 us
    all_gather x1, waiting for transfers between devices, on_device(): cross_block = lax.all_gather(coupling, 'col', axis=0, tiled=True)  57.7 us
    all_to_all x2, waiting for transfers between devices, sum_at_owner(): lax.all_to_all(in_blocks(array, dim, length), axis, 0, 0, tiled=True)  43.2 us
    all_to_all x3, blocking collectives, sent_to_all(): return lax.all_to_all(copies, axis, split_axis=0, concat_axis=0, tiled=True)  39.6 us
    all_gather x1, waiting for transfers between devices, on_device(): first_block = lax.all_gather(inverse_diag[0], 'col', axis=0, tiled=True)  21.5 us
    all_to_all x2, starting transfers between devices, sum_at_owner(): lax.all_to_all(in_blocks(array, dim, length), axis, 0, 0, tiled=True)  16.6 us
    dot_general x4, matrix products, local_product(): lax.dot_general(left_block, right_rows, (((0,), (0,)), ((), ())), preferr...  10.5 us
    all_to_all x2, starting transfers between devices, sent_to_all(): return lax.all_to_all(copies, axis, split_axis=0, concat_axis=0, tiled=True)  10.4 us
  transfers between devices with their start and end apart: 7, of which 6 were waited for; matrix products, arithmetic and copies ran while one was open for 6% of the time, Pallas kernels for 0%

profile of v1, /device:TPU:8, one launch (start us, length us, event | category | flops | bytes accessed | tf_op | source)
XLA Modules:
  0.0 290.3 jit_solution(5077630046471055739)
XLA Ops:
  6.5 1.7 fusion.22
  8.3 0.7 all-gather.6.cloned.1.call-update
  9.0 3.2 %copy.28 = bf16[360,8,2,384]{3,1,2,0:T(8,128)(2,1)S(1)} copy(bf16[360,8,2,384]{3,2,1,0:T(2,128)(2,1)} %bitcast.62) | data formatting | bytes 8847360
  12.2 0.4 slice-done.1
  12.6 4.2 %fusion.23 = f32[768,768]{0,1:T(8,128)S(1)} fusion(bf16[2880,768]{1,0:T(8,128)(2,1)S(1)} %bitcast.63, bf16[2880,768]{1,0:T(8,128)(2,1)S(1)} %bitcast.73), kind=kOutput, calls=%fused_computation.20 | convolution fusion | flops 3397386240 | bytes 11206656 | tf_op jit(solution)/shard_map/dot_general | solution.py:35
  16.8 1.6 fusion.21
  18.4 11.3 %all-to-all-start = ((f32[32,384,24]{1,2,0:T(8,128)}), f32[32,384,24]{1,2,0:T(8,128)S(1)}, u32[]{:S(2)}, u32[]{:S(2)}) async-start(f32[32,384,24]{1,2,0:T(8,128)} %bitcast.2), calls=%async_computation | async-start | bytes 2359296 | tf_op jit(solution)/shard_map/all_to_all | solution.py:15
  29.8 0.7 all-gather.10.cloned.1.call-update
  30.5 0.1 constant_dynamic-slice_fusion
  30.6 0.1 copy.24
  30.7 32.2 %all-to-all-done = f32[32,384,24]{1,2,0:T(8,128)S(1)} async-done(((f32[32,384,24]{1,2,0:T(8,128)}), f32[32,384,24]{1,2,0:T(8,128)S(1)}, u32[]{:S(2)}, u32[]{:S(2)}) %all-to-all-start) | async-done | bytes 1179680 | tf_op jit(solution)/shard_map/all_to_all | solution.py:15
  62.9 0.1 reduce_sum.18
  63.0 9.7 %all_to_all.35 = bf16[8,384,24]{1,2,0:T(8,128)(2,1)S(1)} all-to-all(bf16[8,384,24]{1,2,0:T(8,128)(2,1)S(1)} %broadcast_in_dim.15), channel_id=1, replica_groups=mesh['row'=8,'col'=32] {'row'}, dimensions={0} | all-to-all | bytes 294912 | tf_op jit(solution)/shard_map/all_to_all | solution.py:27
  72.7 5.3 %all-to-all-start.3 = ((f32[32,384,24]{1,2,0:T(8,128)}), f32[32,384,24]{1,2,0:T(8,128)S(1)}, u32[]{:S(2)}, u32[]{:S(2)}) async-start(f32[32,384,24]{1,2,0:T(8,128)} %bitcast.9), calls=%async_computation.3 | async-start | bytes 2359296 | tf_op jit(solution)/shard_map/all_to_all | solution.py:15
  78.1 21.5 %all-gather.8.cloned.1.call-done = bf16[1,3072,384]{2,1,0:T(8,128)(2,1)} async-done(((bf16[1,96,384]{2,1,0:T(8,128)(2,1)}), bf16[1,3072,384]{2,1,0:T(8,128)(2,1)}) %all-gather.8.cloned.1.call-update) | async-done | bytes 2359312 | tf_op jit(solution)/shard_map/all_gather | solution.py:48
  99.6 2.1 fusion.15
  101.7 11.0 %all-to-all-done.3 = f32[32,384,24]{1,2,0:T(8,128)S(1)} async-done(((f32[32,384,24]{1,2,0:T(8,128)}), f32[32,384,24]{1,2,0:T(8,128)S(1)}, u32[]{:S(2)}, u32[]{:S(2)}) %all-to-all-start.3) | async-done | bytes 1179680 | tf_op jit(solution)/shard_map/all_to_all | solution.py:15
  112.8 0.7 broadcast_in_dim.17
  113.5 4.5 %all-to-all-start.4 = ((bf16[8,384,24]{1,2,0:T(8,128)(2,1)}), bf16[8,384,24]{1,2,0:T(8,128)(2,1)S(1)}, u32[]{:S(2)}, u32[]{:S(2)}) async-start(bf16[8,384,24]{1,2,0:T(8,128)(2,1)} %broadcast_in_dim.17), calls=%async_computation.4 | async-start | bytes 294912 | tf_op jit(solution)/shard_map/all_to_all | solution.py:27
  117.9 0.1 reduce_sum.19
  118.0 4.7 %all-to-all-done.4 = bf16[8,384,24]{1,2,0:T(8,128)(2,1)S(1)} async-done(((bf16[8,384,24]{1,2,0:T(8,128)(2,1)}), bf16[8,384,24]{1,2,0:T(8,128)(2,1)S(1)}, u32[]{:S(2)}, u32[]{:S(2)}) %all-to-all-start.4) | async-done | bytes 147488 | tf_op jit(solution)/shard_map/all_to_all | solution.py:27
  122.8 57.7 %all-gather.6.cloned.1.call-done = bf16[3072,384]{1,0:T(8,128)(2,1)} async-done(((bf16[96,384]{1,0:T(8,128)(2,1)}), bf16[3072,384]{1,0:T(8,128)(2,1)}) %all-gather.6.cloned.1.call-update) | async-done | bytes 2359312 | tf_op jit(solution)/shard_map/all_gather | solution.py:49
  180.4 2.1 fusion.5
  182.6 9.4 %all_to_all.36 = bf16[8,384,24]{1,2,0:T(8,128)(2,1)S(1)} all-to-all(bf16[8,384,24]{1,2,0:T(8,128)(2,1)S(1)} %broadcast_in_dim.18), channel_id=1, replica_groups=mesh['row'=8,'col'=32] {'row'}, dimensions={0} | all-to-all | bytes 294912 | tf_op jit(solution)/shard_map/all_to_all | solution.py:27
  192.0 0.9 broadcast_in_dim.16
  192.9 6.0 %all-to-all-start.2 = ((bf16[32,384,24]{1,2,0:T(8,128)(2,1)}), bf16[32,384,24]{1,2,0:T(8,128)(2,1)S(1)}, u32[]{:S(2)}, u32[]{:S(2)}) async-start(bf16[32,384,24]{1,2,0:T(8,128)(2,1)} %broadcast_in_dim.16), calls=%async_computation.2 | async-start | bytes 1179648 | tf_op jit(solution)/shard_map/all_to_all | solution.py:27
  198.9 60.7 %all-gather.10.cloned.1.call-done = bf16[1,3072,384]{2,1,0:T(8,128)(2,1)} async-done(((bf16[1,96,384]{2,1,0:T(8,128)(2,1)}), bf16[1,3072,384]{2,1,0:T(8,128)(2,1)}) %all-gather.10.cloned.1.call-update) | async-done | bytes 2359312 | tf_op jit(solution)/shard_map/all_gather | solution.py:50
  259.6 2.1 fusion.12
  261.7 0.1 broadcast_in_dim.19
  261.7 20.4 %all_to_all.37 = bf16[32,384,24]{1,2,0:T(8,128)(2,1)S(1)} all-to-all(bf16[32,384,24]{1,2,0:T(8,128)(2,1)S(1)} %broadcast_in_dim.19), channel_id=1, replica_groups=mesh['row'=8,'col'=32] {'col'}, dimensions={0} | all-to-all | bytes 1179648 | tf_op jit(solution)/shard_map/all_to_all | solution.py:27
  282.2 0.1 pad_maximum_fusion
  282.3 1.5 copy.23
  (18 shorter events, 0.2 us)
Async XLA Ops:
  6.5 23.9 %copy-start = (bf16[2,384,768]{2,1,0:T(8,128)(2,1)S(1)}, bf16[2,384,768]{2,1,0:T(8,128)(2,1)}, u32[]{:S(2)}) copy-start(bf16[2,384,768]{2,1,0:T(8,128)(2,1)} %param.7) | copy-start | bytes 3538948
  6.5 93.1 %all-gather.8.cloned.1.call-start = ((), (), s32[]{:S(2)}) async-start(), calls=%async_computation.8 | async-start | bytes 2433024 | tf_op jit(solution)/shard_map/all_gather | solution.py:48
  8.2 4.0 %slice-start = ((s8[4423680]{0:T(1024)(128)(4,1)}), s8[229376]{0:T(1024)(128)(4,1)S(1)}, s32[]{:S(2)}) async-start(s8[4423680]{0:T(1024)(128)(4,1)} %bitcast.72), calls=%async_computation.10 | async-start | bytes 458752
  8.3 172.2 %all-gather.6.cloned.1.call-start = ((), (), s32[]{:S(2)}) async-start(), calls=%async_computation.7 | async-start | bytes 2433024 | tf_op jit(solution)/shard_map/all_gather | solution.py:49
  9.0 3.5 %slice-start.1 = ((s8[4423680]{0:T(1024)(128)(4,1)}), s8[4194304]{0:T(1024)(128)(4,1)S(1)}, s32[]{:S(2)}) async-start(s8[4423680]{0:T(1024)(128)(4,1)} %bitcast.72), calls=%async_computation.11 | async-start | bytes 8388608
  18.4 44.5 %all-to-all-start = ((f32[32,384,24]{1,2,0:T(8,128)}), f32[32,384,24]{1,2,0:T(8,128)S(1)}, u32[]{:S(2)}, u32[]{:S(2)}) async-start(f32[32,384,24]{1,2,0:T(8,128)} %bitcast.2), calls=%async_computation | async-start | bytes 2359296 | tf_op jit(solution)/shard_map/all_to_all | solution.py:15
  29.7 229.9 %all-gather.10.cloned.1.call-start = ((), (), s32[]{:S(2)}) async-start(), calls=%async_computation.9 | async-start | bytes 2433024 | tf_op jit(solution)/shard_map/all_gather | solution.py:50
  72.7 40.0 %all-to-all-start.3 = ((f32[32,384,24]{1,2,0:T(8,128)}), f32[32,384,24]{1,2,0:T(8,128)S(1)}, u32[]{:S(2)}, u32[]{:S(2)}) async-start(f32[32,384,24]{1,2,0:T(8,128)} %bitcast.9), calls=%async_computation.3 | async-start | bytes 2359296 | tf_op jit(solution)/shard_map/all_to_all | solution.py:15
  113.5 9.3 %all-to-all-start.4 = ((bf16[8,384,24]{1,2,0:T(8,128)(2,1)}), bf16[8,384,24]{1,2,0:T(8,128)(2,1)S(1)}, u32[]{:S(2)}, u32[]{:S(2)}) async-start(bf16[8,384,24]{1,2,0:T(8,128)(2,1)} %broadcast_in_dim.17), calls=%async_computation.4 | async-start | bytes 294912 | tf_op jit(solution)/shard_map/all_to_all | solution.py:27
  192.9 68.8 %all-to-all-start.2 = ((bf16[32,384,24]{1,2,0:T(8,128)(2,1)}), bf16[32,384,24]{1,2,0:T(8,128)(2,1)S(1)}, u32[]{:S(2)}, u32[]{:S(2)}) async-start(bf16[32,384,24]{1,2,0:T(8,128)(2,1)} %broadcast_in_dim.16), calls=%async_computation.2 | async-start | bytes 1179648 | tf_op jit(solution)/shard_map/all_to_all | solution.py:27
Sparse Core Ops, SparseCore 0:
  9.9 89.6 all-gather.7
  102.2 78.1 all-gather.5
  183.0 76.5 all-gather.9

commit v2 on v1

v2 whole, which is shorter than its diff:
```python
import jax
import jax.numpy as jnp
from jax import lax
from jax.sharding import Mesh, PartitionSpec as P

COL = ("z", "x")


def sent_to_all(array, axis, length):
    copies = jnp.broadcast_to(array, (length, *array.shape))
    return lax.all_to_all(copies, axis, split_axis=0, concat_axis=0, tiled=True)


def left_product(left_block, right_rows):
    return lax.dot_general(
        left_block, right_rows, (((0,), (0,)), ((), ())), preferred_element_type=jnp.float32
    )


def on_device(prior_solved, lower_prior, rhs, coupling, inverse_diag):
    nrow = lax.axis_size("row")
    nz = lax.axis_size("z")
    nx = lax.axis_size("x")
    depth, blocks, rows = lower_prior.shape
    width = rhs.shape[2]
    piece = rows // nz
    quarter = width // nx
    zi = lax.axis_index("z")
    xi = lax.axis_index("x")

    stacked = jnp.stack([inverse_diag[0], coupling, inverse_diag[1]])
    tiles = lax.all_gather(stacked, "x", axis=1, tiled=True)

    both_terms = left_product(lower_prior.reshape(depth, blocks * rows), prior_solved)
    both_terms = both_terms.reshape(blocks, nz, piece, nx, quarter)

    def prior_share(b):
        chunks = jnp.swapaxes(both_terms[b], 1, 2).reshape(nz * nx, piece, quarter)
        return jnp.sum(lax.all_to_all(chunks, COL, 0, 0, tiled=True), axis=0)

    def sum_over_z(partial):
        chunks = partial.reshape(nz, piece, quarter)
        return jnp.sum(lax.all_to_all(chunks, "z", 0, 0, tiled=True), axis=0)

    transpose = [(r * nz + z, z * nz + r) for r in range(nrow) for z in range(nz)]

    def as_input(piece_rows):
        moved = lax.ppermute(piece_rows, ("row", "z"), transpose)
        return sent_to_all(moved, "row", nrow).reshape(rows, quarter)

    rhs_share = lax.dynamic_slice(rhs, (0, zi * piece, xi * quarter), (blocks, piece, quarter))
    rhs_share = rhs_share.astype(jnp.float32)

    first_share = prior_share(0)
    second_share = prior_share(1)
    first_reduced = (rhs_share[0] - first_share).astype(jnp.bfloat16)
    first_solved = sum_over_z(left_product(tiles[0], as_input(first_reduced))).astype(jnp.bfloat16)
    first_out = sent_to_all(first_solved, COL, nz * nx)
    cross_term = sum_over_z(left_product(tiles[1], as_input(first_solved)))
    second_reduced = (rhs_share[1] - second_share - cross_term).astype(jnp.bfloat16)
    second_solved = sum_over_z(left_product(tiles[2], as_input(second_reduced))).astype(jnp.bfloat16)
    second_out = sent_to_all(second_solved, COL, nz * nx)
    out = jnp.stack([first_out, second_out], axis=1)
    out = out.reshape(nz, nx, blocks, piece, quarter)
    return jnp.transpose(out, (2, 0, 3, 1, 4)).reshape(blocks, rows, width)


def solution(mesh):
    nrow, ncol = mesh.devices.shape
    nz = nrow
    fine = Mesh(mesh.devices.reshape(nrow, nz, ncol // nz), ("row", "z", "x"))
    return jax.shard_map(
        on_device,
        mesh=fine,
        in_specs=(
            P(COL, None),
            P(COL, None, "row"),
            P(None, "row", None),
            P(COL, "row"),
            P(None, COL, "row"),
        ),
        out_specs=P(None, "row", None),
        check_vma=False,
    )
```

time: 291 us -> 297 us (1.021)
  waiting for transfers between devices: 189 us -> 132 us
  blocking collectives: 39.6 us -> 79.6 us
  starting transfers between devices: 27.2 us -> 57.8 us
  between operations: 13.3 us -> 0.22 us
  local copies, waits for them, and re-layouts: 10.2 us -> 18 us
  matrix products: 10.5 us -> 5.52 us
    all_gather x3 -> x0, waiting for transfers between devices: 140 us -> none  [the longest x1 60.7 us: on_device(): second_block = lax.all_gather(inverse_diag[1], 'col', axis=0, tiled=True)]
    all_to_all x2 -> x3, waiting for transfers between devices: 43.2 us -> 87.9 us  [the longest x2 75.6 us: prior_share(): return jnp.sum(lax.all_to_all(chunks, COL, 0, 0, tiled=True), axis=0)]
    all_to_all x0 -> x2, blocking collectives: none -> 38.3 us  [sum_over_z(): return jnp.sum(lax.all_to_all(chunks, 'z', 0, 0, tiled=True), axis=0)]
    all_to_all x2 -> x4, waiting for transfers between devices: 4.75 us -> 34.8 us  [sent_to_all(): return lax.all_to_all(copies, axis, split_axis=0, concat_axis=0, tiled=True)]
    all_to_all x2 -> x4, starting transfers between devices: 10.4 us -> 26.4 us  [sent_to_all(): return lax.all_to_all(copies, axis, split_axis=0, concat_axis=0, tiled=True)]
    all_gather x0 -> x1, blocking collectives: none -> 14.2 us  [on_device(): tiles = lax.all_gather(stacked, 'x', axis=1, tiled=True)]
    all_to_all x3 -> x1, blocking collectives: 39.6 us -> 27.1 us  [sent_to_all(): return lax.all_to_all(copies, axis, split_axis=0, concat_axis=0, tiled=True)]
    ppermute x0 -> x3, starting transfers between devices: none -> 9.92 us  [as_input(): moved = lax.ppermute(piece_rows, ('row', 'z'), transpose)]
  transfers between devices with their start and end apart: 7 -> 10, of which waited for: 6 -> 9; matrix products, arithmetic and copies ran while one was open for 6% -> 2% of each run, Pallas kernels for 0% -> 0%
where the time goes in v2:
time: 297 us; the launch traced here: 295 us
  waiting for transfers between devices  132 us (44%)
  blocking collectives  79.6 us (27%)
  starting transfers between devices  57.8 us (19%)
  local copies, waits for them, and re-layouts  18 us (6%)
  matrix products  5.52 us (2%)
    all_to_all x2, waiting for transfers between devices, prior_share(): return jnp.sum(lax.all_to_all(chunks, COL, 0, 0, tiled=True), axis=0)  75.6 us
    all_to_all x2, blocking collectives, sum_over_z(): return jnp.sum(lax.all_to_all(chunks, 'z', 0, 0, tiled=True), axis=0)  38.3 us
    all_to_all x4, waiting for transfers between devices, sent_to_all(): return lax.all_to_all(copies, axis, split_axis=0, concat_axis=0, tiled=True)  34.8 us
    all_to_all x1, blocking collectives, sent_to_all(): return lax.all_to_all(copies, axis, split_axis=0, concat_axis=0, tiled=True)  27.1 us
    all_to_all x4, starting transfers between devices, sent_to_all(): return lax.all_to_all(copies, axis, split_axis=0, concat_axis=0, tiled=True)  26.4 us
    all_to_all x2, starting transfers between devices, prior_share(): return jnp.sum(lax.all_to_all(chunks, COL, 0, 0, tiled=True), axis=0)  17.5 us
    all_gather x1, blocking collectives, on_device(): tiles = lax.all_gather(stacked, 'x', axis=1, tiled=True)  14.2 us
    all_to_all x1, waiting for transfers between devices, sum_over_z(): return jnp.sum(lax.all_to_all(chunks, 'z', 0, 0, tiled=True), axis=0)  12.3 us
  transfers between devices with their start and end apart: 10, of which 9 were waited for; matrix products, arithmetic and copies ran while one was open for 2% of the time, Pallas kernels for 0%

profile of v2, /device:TPU:8, one launch (start us, length us, event | category | flops | bytes accessed | tf_op | source)
XLA Modules:
  0.0 295.2 jit_solution(17263263085924863538)
XLA Ops:
  0.0 3.2 %copy.35 = bf16[360,8,2,384]{3,1,2,0:T(8,128)(2,1)S(1)} copy(bf16[360,8,2,384]{3,2,1,0:T(2,128)(2,1)} %bitcast.59) | data formatting | bytes 8847360
  3.6 4.0 %fusion.7 = f32[768,768]{1,0:T(8,128)S(1)} fusion(bf16[2880,768]{1,0:T(8,128)(2,1)S(1)} %bitcast.60, bf16[2880,768]{1,0:T(8,128)(2,1)S(1)} %copy-done.6), kind=kOutput, calls=%fused_computation.15 | convolution fusion | flops 3397386240 | bytes 11206656 | tf_op jit(solution)/shard_map/dot_general | solution.py:15
  7.6 1.2 fusion.5
  8.8 2.4 squeeze.23
  11.1 1.4 copy.21
  12.6 11.4 %all-to-all-start = ((f32[32,48,192]{2,1,0:T(8,128)}), f32[32,48,192]{2,1,0:T(8,128)S(1)}, u32[]{:S(2)}, u32[]{:S(2)}) async-start(f32[32,48,192]{2,1,0:T(8,128)} %bitcast.6), calls=%async_computation | async-start | bytes 3145728 | tf_op jit(solution)/shard_map/all_to_all | solution.py:39
  25.1 38.0 %all-to-all-done = f32[32,48,192]{2,1,0:T(8,128)S(1)} async-done(((f32[32,48,192]{2,1,0:T(8,128)}), f32[32,48,192]{2,1,0:T(8,128)S(1)}, u32[]{:S(2)}, u32[]{:S(2)}) %all-to-all-start) | async-done | bytes 1179680 | tf_op jit(solution)/shard_map/all_to_all | solution.py:39
  63.3 4.5 %collective-permute-start = (bf16[48,192]{1,0:T(8,128)(2,1)S(1)}, bf16[48,192]{1,0:T(8,128)(2,1)S(1)}, u32[]{:S(2)}, u32[]{:S(2)}) collective-permute-start(bf16[48,192]{1,0:T(8,128)(2,1)S(1)} %fusion.4), channel_id=1, source_target_pairs={{0,0},{4,32},{8,64},{12,96},{16,128},{20,160},{24,192},{28,224},{3... | collective-permute-start | bytes 55304 | tf_op jit(solution)/shard_map/ppermute | solution.py:48
  67.8 14.2 %all_gather.3 = bf16[3,384,384]{2,1,0:T(8,128)(2,1)S(1)} all-gather(bf16[3,96,384]{2,1,0:T(8,128)(2,1)S(1)} %pad_maximum_fusion), channel_id=1, replica_groups=mesh['row'=8,'z'=8,'x'=4] {'x'}, dimensions={1}, use_global_device_ids=true | all-gather | bytes 1105920 | tf_op jit(solution)/shard_map/all_gather | solution.py:32
  82.7 4.7 %all-to-all-start.1 = ((bf16[8,48,192]{2,1,0:T(8,128)(2,1)}), bf16[8,48,192]{2,1,0:T(8,128)(2,1)S(1)}, u32[]{:S(2)}, u32[]{:S(2)}) async-start(bf16[8,48,192]{2,1,0:T(8,128)(2,1)} %broadcast_in_dim.15), calls=%async_computation.1 | async-start | bytes 393216 | tf_op jit(solution)/shard_map/all_to_all | solution.py:11
  87.7 5.0 %all-to-all-done.1 = bf16[8,48,192]{2,1,0:T(8,128)(2,1)S(1)} async-done(((bf16[8,48,192]{2,1,0:T(8,128)(2,1)}), bf16[8,48,192]{2,1,0:T(8,128)(2,1)S(1)}, u32[]{:S(2)}, u32[]{:S(2)}) %all-to-all-start.1) | async-done | bytes 147488 | tf_op jit(solution)/shard_map/all_to_all | solution.py:11
  93.0 21.1 %all_to_all.50 = f32[8,48,192]{2,1,0:T(8,128)S(1)} all-to-all(f32[8,48,192]{2,1,0:T(8,128)S(1)} %fusion.8), channel_id=1, replica_groups=mesh['row'=8,'z'=8,'x'=4] {'z'}, dimensions={0} | all-to-all | bytes 589824 | tf_op jit(solution)/shard_map/all_to_all | solution.py:43
  114.1 2.9 collective-permute-start.1
  117.0 4.7 %collective-permute-done.1 = bf16[48,192]{1,0:T(8,128)(2,1)S(1)} collective-permute-done((bf16[48,192]{1,0:T(8,128)(2,1)S(1)}, bf16[48,192]{1,0:T(8,128)(2,1)S(1)}, u32[]{:S(2)}, u32[]{:S(2)}) %collective-permute-start.1) | collective-permute-done | bytes 18464 | tf_op jit(solution)/shard_map/ppermute | solution.py:48
  122.3 7.9 %all-to-all-start.5 = ((bf16[8,48,192]{2,1,0:T(8,128)(2,1)}), bf16[8,48,192]{2,1,0:T(8,128)(2,1)S(1)}, u32[]{:S(2)}, u32[]{:S(2)}) async-start(bf16[8,48,192]{2,1,0:T(8,128)(2,1)} %broadcast_in_dim.17), calls=%async_computation.5 | async-start | bytes 393216 | tf_op jit(solution)/shard_map/all_to_all | solution.py:11
  130.3 1.2 squeeze.26
  131.4 1.4 copy.24
  132.9 2.7 all-to-all-done.5
  135.6 6.0 %all-to-all-start.4 = ((f32[32,48,192]{2,1,0:T(8,128)}), f32[32,48,192]{2,1,0:T(8,128)S(1)}, u32[]{:S(2)}, u32[]{:S(2)}) async-start(f32[32,48,192]{2,1,0:T(8,128)} %bitcast.15), calls=%async_computation.4 | async-start | bytes 3145728 | tf_op jit(solution)/shard_map/all_to_all | solution.py:39
  141.9 1.0 fusion.9
  142.9 37.6 %all-to-all-done.4 = f32[32,48,192]{2,1,0:T(8,128)S(1)} async-done(((f32[32,48,192]{2,1,0:T(8,128)}), f32[32,48,192]{2,1,0:T(8,128)S(1)}, u32[]{:S(2)}, u32[]{:S(2)}) %all-to-all-start.4) | async-done | bytes 1179680 | tf_op jit(solution)/shard_map/all_to_all | solution.py:39
  180.5 4.0 %all-to-all-start.6 = ((f32[8,48,192]{2,1,0:T(8,128)}), f32[8,48,192]{2,1,0:T(8,128)S(1)}, u32[]{:S(2)}, u32[]{:S(2)}) async-start(f32[8,48,192]{2,1,0:T(8,128)} %fusion.9), calls=%async_computation.6 | async-start | bytes 786432 | tf_op jit(solution)/shard_map/all_to_all | solution.py:43
  184.6 12.3 %all-to-all-done.6 = f32[8,48,192]{2,1,0:T(8,128)S(1)} async-done(((f32[8,48,192]{2,1,0:T(8,128)}), f32[8,48,192]{2,1,0:T(8,128)S(1)}, u32[]{:S(2)}, u32[]{:S(2)}) %all-to-all-start.6) | async-done | bytes 294944 | tf_op jit(solution)/shard_map/all_to_all | solution.py:43
  197.0 2.6 collective-permute-start.2
  199.6 4.9 %collective-permute-done.2 = bf16[48,192]{1,0:T(8,128)(2,1)S(1)} collective-permute-done((bf16[48,192]{1,0:T(8,128)(2,1)S(1)}, bf16[48,192]{1,0:T(8,128)(2,1)S(1)}, u32[]{:S(2)}, u32[]{:S(2)}) %collective-permute-start.2) | collective-permute-done | bytes 18464 | tf_op jit(solution)/shard_map/ppermute | solution.py:48
  205.2 8.1 %all-to-all-start.7 = ((bf16[8,48,192]{2,1,0:T(8,128)(2,1)}), bf16[8,48,192]{2,1,0:T(8,128)(2,1)S(1)}, u32[]{:S(2)}, u32[]{:S(2)}) async-start(bf16[8,48,192]{2,1,0:T(8,128)(2,1)} %broadcast_in_dim.18), calls=%async_computation.7 | async-start | bytes 393216 | tf_op jit(solution)/shard_map/all_to_all | solution.py:11
  213.5 5.1 %all-to-all-done.7 = bf16[8,48,192]{2,1,0:T(8,128)(2,1)S(1)} async-done(((bf16[8,48,192]{2,1,0:T(8,128)(2,1)}), bf16[8,48,192]{2,1,0:T(8,128)(2,1)S(1)}, u32[]{:S(2)}, u32[]{:S(2)}) %all-to-all-start.7) | async-done | bytes 147488 | tf_op jit(solution)/shard_map/all_to_all | solution.py:11
  218.9 17.2 %all_to_all.51 = f32[8,48,192]{2,1,0:T(8,128)S(1)} all-to-all(f32[8,48,192]{2,1,0:T(8,128)S(1)} %fusion.10), channel_id=1, replica_groups=mesh['row'=8,'z'=8,'x'=4] {'z'}, dimensions={0} | all-to-all | bytes 589824 | tf_op jit(solution)/shard_map/all_to_all | solution.py:43
  237.1 5.7 %all-to-all-start.3 = ((bf16[32,48,192]{2,1,0:T(8,128)(2,1)}), bf16[32,48,192]{2,1,0:T(8,128)(2,1)S(1)}, u32[]{:S(2)}, u32[]{:S(2)}) async-start(bf16[32,48,192]{2,1,0:T(8,128)(2,1)} %broadcast_in_dim.16), calls=%async_computation.3 | async-start | bytes 1572864 | tf_op jit(solution)/shard_map/all_to_all | solution.py:11
  242.8 21.9 %all-to-all-done.3 = bf16[32,48,192]{2,1,0:T(8,128)(2,1)S(1)} async-done(((bf16[32,48,192]{2,1,0:T(8,128)(2,1)}), bf16[32,48,192]{2,1,0:T(8,128)(2,1)S(1)}, u32[]{:S(2)}, u32[]{:S(2)}) %all-to-all-start.3) | async-done | bytes 589856 | tf_op jit(solution)/shard_map/all_to_all | solution.py:11
  264.7 27.1 %all_to_all.52 = bf16[32,48,192]{2,1,0:T(8,128)(2,1)S(1)} all-to-all(bf16[32,48,192]{2,1,0:T(8,128)(2,1)S(1)} %broadcast_in_dim.19), channel_id=1, replica_groups=mesh['row'=8,'z'=8,'x'=4] {'z','x'}, dimensions={0} | all-to-all | bytes 1179648 | tf_op jit(solution)/shard_map/all_to_all | solution.py:11
  292.9 2.2 reshape.43
  (38 shorter events, 7.2 us)
Async XLA Ops:
  0.0 3.6 %copy-start.6 = (bf16[2880,768]{1,0:T(8,128)(2,1)S(1)}, bf16[2880,768]{1,0:T(8,128)(2,1)}, u32[]{:S(2)}) copy-start(bf16[2880,768]{1,0:T(8,128)(2,1)} %param.5) | copy-start | bytes 13271044
  12.6 12.5 %copy-start.2 = (bf16[2,96,384]{2,1,0:T(8,128)(2,1)S(1)}, bf16[2,96,384]{2,1,0:T(8,128)(2,1)}, u32[]{:S(2)}) copy-start(bf16[2,96,384]{2,1,0:T(8,128)(2,1)} %param.9) | copy-start | bytes 442372
  12.6 12.5 %copy-start.5 = (bf16[96,384]{1,0:T(8,128)(2,1)S(1)}, bf16[96,384]{1,0:T(8,128)(2,1)}, u32[]{:S(2)}) copy-start(bf16[96,384]{1,0:T(8,128)(2,1)} %param.8) | copy-start | bytes 221188
  12.6 50.6 %all-to-all-start = ((f32[32,48,192]{2,1,0:T(8,128)}), f32[32,48,192]{2,1,0:T(8,128)S(1)}, u32[]{:S(2)}, u32[]{:S(2)}) async-start(f32[32,48,192]{2,1,0:T(8,128)} %bitcast.6), calls=%async_computation | async-start | bytes 3145728 | tf_op jit(solution)/shard_map/all_to_all | solution.py:39
  25.1 56.9 %copy-start = (f32[2,48,192]{2,1,0:T(8,128)}, f32[2,48,192]{2,1,0:T(8,128)S(1)}, u32[]{:S(2)}) copy-start(f32[2,48,192]{2,1,0:T(8,128)S(1)} %dynamic-slice_convert_fusion) | copy-start | bytes 221188
  63.3 18.7 %collective-permute-start = (bf16[48,192]{1,0:T(8,128)(2,1)S(1)}, bf16[48,192]{1,0:T(8,128)(2,1)S(1)}, u32[]{:S(2)}, u32[]{:S(2)}) collective-permute-start(bf16[48,192]{1,0:T(8,128)(2,1)S(1)} %fusion.4), channel_id=1, source_target_pairs={{0,0},{4,32},{8,64},{12,96},{16,128},{20,160},{24,192},{28,224},{3... | collective-permute-start | bytes 55304 | tf_op jit(solution)/shard_map/ppermute | solution.py:48
  82.7 10.1 %all-to-all-start.1 = ((bf16[8,48,192]{2,1,0:T(8,128)(2,1)}), bf16[8,48,192]{2,1,0:T(8,128)(2,1)S(1)}, u32[]{:S(2)}, u32[]{:S(2)}) async-start(bf16[8,48,192]{2,1,0:T(8,128)(2,1)} %broadcast_in_dim.15), calls=%async_computation.1 | async-start | bytes 393216 | tf_op jit(solution)/shard_map/all_to_all | solution.py:11
  114.1 16.2 %copy-start.3 = (bf16[48,192]{1,0:T(8,128)(2,1)}, bf16[48,192]{1,0:T(8,128)(2,1)S(1)}, u32[]{:S(2)}) copy-start(bf16[48,192]{1,0:T(8,128)(2,1)S(1)} %reduce_sum.46) | copy-start | bytes 55300
  114.1 7.5 %collective-permute-start.1 = (bf16[48,192]{1,0:T(8,128)(2,1)S(1)}, bf16[48,192]{1,0:T(8,128)(2,1)S(1)}, u32[]{:S(2)}, u32[]{:S(2)}) collective-permute-start(bf16[48,192]{1,0:T(8,128)(2,1)S(1)} %reduce_sum.46), channel_id=1, source_target_pairs={{0,0},{4,32},{8,64},{12,96},{16,128},{20,160},{24,192},{28,224},{3... | collective-permute-start | bytes 55304 | tf_op jit(solution)/shard_map/ppermute | solution.py:48
  122.3 13.3 %all-to-all-start.5 = ((bf16[8,48,192]{2,1,0:T(8,128)(2,1)}), bf16[8,48,192]{2,1,0:T(8,128)(2,1)S(1)}, u32[]{:S(2)}, u32[]{:S(2)}) async-start(bf16[8,48,192]{2,1,0:T(8,128)(2,1)} %broadcast_in_dim.17), calls=%async_computation.5 | async-start | bytes 393216 | tf_op jit(solution)/shard_map/all_to_all | solution.py:11
  135.6 44.9 %all-to-all-start.4 = ((f32[32,48,192]{2,1,0:T(8,128)}), f32[32,48,192]{2,1,0:T(8,128)S(1)}, u32[]{:S(2)}, u32[]{:S(2)}) async-start(f32[32,48,192]{2,1,0:T(8,128)} %bitcast.15), calls=%async_computation.4 | async-start | bytes 3145728 | tf_op jit(solution)/shard_map/all_to_all | solution.py:39
  142.9 54.1 %copy-start.1 = (f32[2,48,192]{2,1,0:T(8,128)S(1)}, f32[2,48,192]{2,1,0:T(8,128)}, u32[]{:S(2)}) copy-start(f32[2,48,192]{2,1,0:T(8,128)} %copy-done) | copy-start | bytes 221188
  180.5 16.4 %all-to-all-start.6 = ((f32[8,48,192]{2,1,0:T(8,128)}), f32[8,48,192]{2,1,0:T(8,128)S(1)}, u32[]{:S(2)}, u32[]{:S(2)}) async-start(f32[8,48,192]{2,1,0:T(8,128)} %fusion.9), calls=%async_computation.6 | async-start | bytes 786432 | tf_op jit(solution)/shard_map/all_to_all | solution.py:43
  197.0 39.2 %copy-start.4 = (bf16[48,192]{1,0:T(8,128)(2,1)S(1)}, bf16[48,192]{1,0:T(8,128)(2,1)}, u32[]{:S(2)}) copy-start(bf16[48,192]{1,0:T(8,128)(2,1)} %copy-done.3) | copy-start | bytes 55300
  197.0 7.5 %collective-permute-start.2 = (bf16[48,192]{1,0:T(8,128)(2,1)S(1)}, bf16[48,192]{1,0:T(8,128)(2,1)S(1)}, u32[]{:S(2)}, u32[]{:S(2)}) collective-permute-start(bf16[48,192]{1,0:T(8,128)(2,1)S(1)} %fusion.2), channel_id=1, source_target_pairs={{0,0},{4,32},{8,64},{12,96},{16,128},{20,160},{24,192},{28,224},{3... | collective-permute-start | bytes 55304 | tf_op jit(solution)/shard_map/ppermute | solution.py:48
  205.2 13.4 %all-to-all-start.7 = ((bf16[8,48,192]{2,1,0:T(8,128)(2,1)}), bf16[8,48,192]{2,1,0:T(8,128)(2,1)S(1)}, u32[]{:S(2)}, u32[]{:S(2)}) async-start(bf16[8,48,192]{2,1,0:T(8,128)(2,1)} %broadcast_in_dim.18), calls=%async_computation.7 | async-start | bytes 393216 | tf_op jit(solution)/shard_map/all_to_all | solution.py:11
  237.1 27.6 %all-to-all-start.3 = ((bf16[32,48,192]{2,1,0:T(8,128)(2,1)}), bf16[32,48,192]{2,1,0:T(8,128)(2,1)S(1)}, u32[]{:S(2)}, u32[]{:S(2)}) async-start(bf16[32,48,192]{2,1,0:T(8,128)(2,1)} %broadcast_in_dim.16), calls=%async_computation.3 | async-start | bytes 1572864 | tf_op jit(solution)/shard_map/all_to_all | solution.py:11

commit v3 on v2

v3 whole, which is shorter than its diff:
```python
import jax
import jax.numpy as jnp
from jax import lax
from jax.sharding import Mesh, PartitionSpec as P

COL = ("z", "x")


def sent_to_all(array, axis, length):
    copies = jnp.broadcast_to(array, (length, *array.shape))
    return lax.all_to_all(copies, axis, split_axis=0, concat_axis=0, tiled=True)


def left_product(left_block, right_rows):
    return lax.dot_general(
        left_block, right_rows, (((0,), (0,)), ((), ())), preferred_element_type=jnp.float32
    )


def on_device(prior_solved, lower_prior, rhs, coupling, inverse_diag):
    nrow = lax.axis_size("row")
    nz = lax.axis_size("z")
    nx = lax.axis_size("x")
    ncol = nz * nx
    depth, blocks, rows = lower_prior.shape
    width = rhs.shape[2]
    piece = rows // nz
    quarter = width // nx
    share = quarter // nz
    zi = lax.axis_index("z")
    xi = lax.axis_index("x")

    later_blocks = lax.all_gather(jnp.stack([coupling, inverse_diag[1]]), COL, axis=1, tiled=True)
    first_tile = lax.all_gather(inverse_diag[0], "x", axis=0, tiled=True)

    both_terms = left_product(lower_prior.reshape(depth, blocks * rows), prior_solved)
    both_terms = both_terms.reshape(blocks, rows, width).astype(jnp.bfloat16)
    first_chunks = both_terms[0].reshape(nz, piece, nx, quarter).transpose(0, 2, 1, 3)
    second_chunks = both_terms[1].reshape(rows, nx, nz, share).transpose(2, 1, 0, 3)
    chunks = jnp.concatenate(
        [first_chunks.reshape(ncol, piece * quarter), second_chunks.reshape(ncol, rows * share)], axis=1
    )
    sums = jnp.sum(lax.all_to_all(chunks, COL, 0, 0, tiled=True).astype(jnp.float32), axis=0)
    first_share = sums[: piece * quarter].reshape(piece, quarter)
    second_share = sums[piece * quarter :].reshape(rows, share)

    rhs_first = lax.dynamic_slice(rhs[0], (zi * piece, xi * quarter), (piece, quarter))
    rhs_second = lax.dynamic_slice(rhs[1], (0, xi * quarter + zi * share), (rows, share))

    transpose = [(r * nz + z, z * nz + r) for r in range(nrow) for z in range(nz)]

    def as_tile_input(piece_rows):
        moved = lax.ppermute(piece_rows, ("row", "z"), transpose)
        return sent_to_all(moved, "row", nrow).reshape(rows, quarter)

    def as_full_input(share_rows):
        return sent_to_all(share_rows, "row", nrow).reshape(nrow * rows, share)

    def output_rows(share_rows):
        got = sent_to_all(share_rows, COL, ncol).reshape(nz, nx, rows, share)
        return got.transpose(2, 1, 0, 3).reshape(rows, width)

    first_reduced = (rhs_first.astype(jnp.float32) - first_share).astype(jnp.bfloat16)
    partial = left_product(first_tile, as_tile_input(first_reduced)).reshape(nz, piece, quarter)
    first_piece = jnp.sum(lax.all_to_all(partial, "z", 0, 0, tiled=True), axis=0).astype(jnp.bfloat16)
    split = first_piece.reshape(piece, nz, share).transpose(1, 0, 2)
    first_solved = lax.all_to_all(split, "z", 0, 0, tiled=True).reshape(rows, share)
    first_out = output_rows(first_solved)

    cross_term = left_product(later_blocks[0], as_full_input(first_solved))
    second_reduced = (rhs_second.astype(jnp.float32) - second_share - cross_term).astype(jnp.bfloat16)
    second_solved = left_product(later_blocks[1], as_full_input(second_reduced)).astype(jnp.bfloat16)
    second_out = output_rows(second_solved)
    return jnp.stack([first_out, second_out])


def solution(mesh):
    nrow, ncol = mesh.devices.shape
    nz = nrow
    fine = Mesh(mesh.devices.reshape(nrow, nz, ncol // nz), ("row", "z", "x"))
    return jax.shard_map(
        on_device,
        mesh=fine,
        in_specs=(
            P(COL, None),
            P(COL, None, "row"),
            P(None, "row", None),
            P(COL, "row"),
            P(None, COL, "row"),
        ),
        out_specs=P(None, "row", None),
        check_vma=False,
    )
```

time: 297 us -> 243 us (0.82)
  waiting for transfers between devices: 132 us -> 86.1 us
  blocking collectives: 79.6 us -> 46.7 us
  local copies, waits for them, and re-layouts: 18 us -> 39.9 us
  starting transfers between devices: 57.8 us -> 36.6 us
  between operations: 0.22 us -> 13.7 us
  matrix products: 5.52 us -> 12 us
  other arithmetic: 1.67 us -> 6.69 us
    all_to_all x3 -> x1, waiting for transfers between devices: 87.9 us -> 42 us  [on_device(): lax.all_to_all(chunks, COL, 0, 0, tiled=True).astype(jnp.float32)]
    all_to_all x1, blocking collectives: 27.1 us -> 8.67 us  [sent_to_all(): return lax.all_to_all(copies, axis, split_axis=0, concat_axis=0, tiled=True)]
    all_to_all x2, blocking collectives: 38.3 us -> 25.4 us  [the longest x1 15.3 us: on_device(): lax.all_to_all(partial, 'z', 0, 0, tiled=True)]
    dot_general x4 -> x2, local copies, waits for them, and re-layouts: 0.74 us -> 12.6 us  [left_product(): lax.dot_general(left_block, right_rows, (((0,), (0,)), ((), ())), preferr...]
    all_to_all x3 -> x1, starting transfers between devices: 21.5 us -> 11.7 us  [on_device(): lax.all_to_all(chunks, COL, 0, 0, tiled=True).astype(jnp.float32)]
    ppermute x3 -> x1, starting transfers between devices: 9.92 us -> 1.91 us  [as_tile_input(): moved = lax.ppermute(piece_rows, ('row', 'z'), transpose)]
    dot_general x4, matrix products: 5.52 us -> 12 us  [left_product(): lax.dot_general(left_block, right_rows, (((0,), (0,)), ((), ())), preferr...]
    squeeze x4 -> x0, local copies, waits for them, and re-layouts: 6.4 us -> none  [prior_share(): chunks = jnp.swapaxes(both_terms[b], 1, 2).reshape(nz * nx, piece, quarter)]
  transfers between devices with their start and end apart: 10 -> 7, of which waited for: 9 -> 5; matrix products, arithmetic and copies ran while one was open for 2% -> 21% of each run, Pallas kernels for 0% -> 0%
where the time goes in v3:
time: 243 us; the launch traced here: 242 us
  waiting for transfers between devices  86.1 us (35%)
  blocking collectives  46.7 us (19%)
  local copies, waits for them, and re-layouts  39.9 us (16%)
  starting transfers between devices  36.6 us (15%)
  between operations  13.7 us (6%)
  matrix products  12 us (5%)
  other arithmetic  6.69 us (3%)
    all_to_all x1, waiting for transfers between devices, on_device(): lax.all_to_all(chunks, COL, 0, 0, tiled=True).astype(jnp.float32)  42 us
    all_to_all x4, waiting for transfers between devices, sent_to_all(): return lax.all_to_all(copies, axis, split_axis=0, concat_axis=0, tiled=True)  38.4 us
    all_to_all x4, starting transfers between devices, sent_to_all(): return lax.all_to_all(copies, axis, split_axis=0, concat_axis=0, tiled=True)  23 us
    all_to_all x1, blocking collectives, on_device(): lax.all_to_all(partial, 'z', 0, 0, tiled=True)  15.3 us
    all_gather x1, blocking collectives, on_device(): first_tile = lax.all_gather(inverse_diag[0], 'x', axis=0, tiled=True)  12.6 us
    dot_general x2, local copies, waits for them, and re-layouts, left_product(): lax.dot_general(left_block, right_rows, (((0,), (0,)), ((), ())), preferr...  12.6 us
    dot_general x4, matrix products, left_product(): lax.dot_general(left_block, right_rows, (((0,), (0,)), ((), ())), preferr...  12 us
    all_to_all x1, starting transfers between devices, on_device(): lax.all_to_all(chunks, COL, 0, 0, tiled=True).astype(jnp.float32)  11.7 us
  transfers between devices with their start and end apart: 7, of which 5 were waited for; matrix products, arithmetic and copies ran while one was open for 21% of the time, Pallas kernels for 0%

profile of v3, /device:TPU:8, one launch (start us, length us, event | category | flops | bytes accessed | tf_op | source)
XLA Modules:
  0.0 241.6 jit_solution(10142438685066964138)
XLA Ops:
  6.5 1.6 fusion.17
  8.1 1.6 pad_maximum_fusion.1
  9.7 12.4 %copy.56 = bf16[2880,2,384]{0,2,1:T(8,128)(2,1)} copy(bf16[2880,2,384]{2,1,0:T(2,128)(2,1)} %param.6) | data formatting | bytes 8847360 | tf_op jit(solution)/shard_map/dot_general | solution.py:15
  22.1 7.5 %fusion.5 = bf16[2,384,768]{2,1,0:T(8,128)(2,1)S(1)} fusion(bf16[2880,768]{1,0:T(8,128)(2,1)} %param.5, bf16[2880,2,384]{0,2,1:T(8,128)(2,1)} %copy.56), kind=kOutput, calls=%fused_computation.8 | convolution fusion | flops 3397976064 | bytes 10027008 | tf_op jit(solution)/shard_map/dot_general | solution.py:15
  30.6 1.1 copy.40
  31.6 2.8 %copy.41 = bf16[8,4,384,24]{3,2,1,0:T(8,128)(2,1)S(1)} copy(bf16[8,4,384,24]{2,3,0,1:T(8,128)(2,1)} %bitcast.75) | data formatting | bytes 1179648 | tf_op jit(solution)/shard_map/transpose | solution.py:39
  34.5 6.7 %reshape.66 = bf16[32,9216]{1,0:T(8,128)(2,1)} reshape(bf16[8,4,384,24]{3,2,1,0:T(8,128)(2,1)S(1)} %copy.41) | data formatting | bytes 1179648 | tf_op jit(solution)/shard_map/reshape | solution.py:41
  41.2 2.3 reshape_squeeze.6
  45.1 1.6 reduce.1
  46.7 1.7 reshape.79
  48.4 11.7 %all-to-all-start = ((bf16[32,2,9216]{2,1,0:T(2,128)(2,1)}), bf16[32,2,9216]{2,1,0:T(2,128)(2,1)S(1)}, u32[]{:S(2)}, u32[]{:S(2)}) async-start(bf16[32,2,9216]{2,1,0:T(2,128)(2,1)} %reshape.79), calls=%async_computation | async-start | bytes 2359296 | tf_op jit(solution)/shard_map/all_to_all | solution.py:43
  60.1 1.1 fusion.15
  61.3 42.0 %all-to-all-done = bf16[32,2,9216]{2,1,0:T(2,128)(2,1)S(1)} async-done(((bf16[32,2,9216]{2,1,0:T(2,128)(2,1)}), bf16[32,2,9216]{2,1,0:T(2,128)(2,1)S(1)}, u32[]{:S(2)}, u32[]{:S(2)}) %all-to-all-start) | async-done | bytes 1179680 | tf_op jit(solution)/shard_map/all_to_all | solution.py:43
  103.3 1.0 reshape.80
  104.2 2.5 %convert_reduce_fusion = f32[18432]{0:T(1024)S(1)} fusion(bf16[32,1,18432]{2,1,0:T(2,128)(2,1)S(1)} %reshape.80), kind=kLoop, calls=%fused_computation.7 | loop fusion | flops 1161216 | bytes 1253376 | tf_op jit(solution)/shard_map/reduce_sum | solution.py:43
  107.7 1.9 collective-permute-start
  109.6 5.6 %collective-permute-done = bf16[48,192]{1,0:T(8,128)(2,1)S(1)} collective-permute-done((bf16[48,192]{1,0:T(8,128)(2,1)S(1)}, bf16[48,192]{1,0:T(8,128)(2,1)S(1)}, u32[]{:S(2)}, u32[]{:S(2)}) %collective-permute-start) | collective-permute-done | bytes 18464 | tf_op jit(solution)/shard_map/ppermute | solution.py:53
  115.9 9.4 %all-to-all-start.1 = ((bf16[8,48,192]{2,1,0:T(8,128)(2,1)}), bf16[8,48,192]{2,1,0:T(8,128)(2,1)S(1)}, u32[]{:S(2)}, u32[]{:S(2)}) async-start(bf16[8,48,192]{2,1,0:T(8,128)(2,1)} %broadcast_in_dim.15), calls=%async_computation.1 | async-start | bytes 393216 | tf_op jit(solution)/shard_map/all_to_all | solution.py:11
  125.3 12.6 %all-gather = bf16[1,384,384]{2,1,0:T(8,128)(2,1)S(1)} all-gather(bf16[1,96,384]{2,1,0:T(8,128)(2,1)S(1)} %copy-done.2), channel_id=2, replica_groups=mesh['row'=8,'z'=8,'x'=4] {'x'}, dimensions={1}, use_global_device_ids=true | all-gather | bytes 368640 | tf_op jit(solution)/shard_map/all_gather | solution.py:34
  138.4 15.3 %all_to_all.44 = f32[8,48,192]{2,1,0:T(8,128)S(1)} all-to-all(f32[8,48,192]{2,1,0:T(8,128)S(1)} %bitcast.80), channel_id=1, replica_groups=mesh['row'=8,'z'=8,'x'=4] {'z'}, dimensions={0} | all-to-all | bytes 589824 | tf_op jit(solution)/shard_map/all_to_all | solution.py:65
  153.9 10.2 %all_to_all.45 = bf16[8,2,576]{2,1,0:T(2,128)(2,1)S(1)} all-to-all(bf16[8,2,576]{2,1,0:T(2,128)(2,1)S(1)} %reshape.81), channel_id=1, replica_groups=mesh['row'=8,'z'=8,'x'=4] {'z'}, dimensions={0} | all-to-all | bytes 36864 | tf_op jit(solution)/shard_map/all_to_all | solution.py:67
  165.0 4.8 %all-to-all-start.5 = ((bf16[8,384,24]{1,2,0:T(8,128)(2,1)}), bf16[8,384,24]{1,2,0:T(8,128)(2,1)S(1)}, u32[]{:S(2)}, u32[]{:S(2)}) async-start(bf16[8,384,24]{1,2,0:T(8,128)(2,1)} %broadcast_in_dim.17), calls=%async_computation.5 | async-start | bytes 294912 | tf_op jit(solution)/shard_map/all_to_all | solution.py:11
  169.8 1.0 constant_dynamic-slice_fusion
  171.2 3.5 %all-to-all-done.5 = bf16[8,384,24]{1,2,0:T(8,128)(2,1)S(1)} async-done(((bf16[8,384,24]{1,2,0:T(8,128)(2,1)}), bf16[8,384,24]{1,2,0:T(8,128)(2,1)S(1)}, u32[]{:S(2)}, u32[]{:S(2)}) %all-to-all-start.5) | async-done | bytes 147488 | tf_op jit(solution)/shard_map/all_to_all | solution.py:11
  174.7 2.1 fusion.11
  176.8 8.7 %all_to_all.46 = bf16[8,384,24]{1,2,0:T(8,128)(2,1)S(1)} all-to-all(bf16[8,384,24]{1,2,0:T(8,128)(2,1)S(1)} %broadcast_in_dim.18), channel_id=1, replica_groups=mesh['row'=8,'z'=8,'x'=4] {'row'}, dimensions={0} | all-to-all | bytes 294912 | tf_op jit(solution)/shard_map/all_to_all | solution.py:11
  186.3 3.9 %all-to-all-start.4 = ((bf16[32,384,24]{1,2,0:T(8,128)(2,1)}), bf16[32,384,24]{1,2,0:T(8,128)(2,1)S(1)}, u32[]{:S(2)}, u32[]{:S(2)}) async-start(bf16[32,384,24]{1,2,0:T(8,128)(2,1)} %broadcast_in_dim.16), calls=%async_computation.4 | async-start | bytes 1179648 | tf_op jit(solution)/shard_map/all_to_all | solution.py:11
  190.3 2.1 fusion.12
  192.4 16.9 %all-to-all-done.4 = bf16[32,384,24]{1,2,0:T(8,128)(2,1)S(1)} async-done(((bf16[32,384,24]{1,2,0:T(8,128)(2,1)}), bf16[32,384,24]{1,2,0:T(8,128)(2,1)S(1)}, u32[]{:S(2)}, u32[]{:S(2)}) %all-to-all-start.4) | async-done | bytes 589856 | tf_op jit(solution)/shard_map/all_to_all | solution.py:11
  210.1 4.9 %all-to-all-start.7 = ((bf16[32,384,24]{1,2,0:T(8,128)(2,1)}), bf16[32,384,24]{1,2,0:T(8,128)(2,1)S(1)}, u32[]{:S(2)}, u32[]{:S(2)}) async-start(bf16[32,384,24]{1,2,0:T(8,128)(2,1)} %broadcast_in_dim.19), calls=%async_computation.7 | async-start | bytes 1179648 | tf_op jit(solution)/shard_map/all_to_all | solution.py:11
  215.0 18.1 %all-to-all-done.7 = bf16[32,384,24]{1,2,0:T(8,128)(2,1)S(1)} async-done(((bf16[32,384,24]{1,2,0:T(8,128)(2,1)}), bf16[32,384,24]{1,2,0:T(8,128)(2,1)S(1)}, u32[]{:S(2)}, u32[]{:S(2)}) %all-to-all-start.7) | async-done | bytes 589856 | tf_op jit(solution)/shard_map/all_to_all | solution.py:11
  233.3 1.5 copy.52
  (39 shorter events, 8.1 us)
Async XLA Ops:
  6.5 168.1 %all-gather.3.cloned.1.call-start = ((), (), s32[]{:S(2)}) async-start(), calls=%async_computation.8 | async-start | bytes 4866048 | tf_op jit(solution)/shard_map/all_gather | solution.py:33
  41.2 3.3 %copy-start = (bf16[32,9216]{1,0:T(8,128)(2,1)S(1)}, bf16[32,9216]{1,0:T(8,128)(2,1)}, u32[]{:S(2)}) copy-start(bf16[32,9216]{1,0:T(8,128)(2,1)} %reshape.66) | copy-start | bytes 1769476
  48.4 11.7 %copy-start.1 = (bf16[2,384,768]{2,1,0:T(8,128)(2,1)S(1)}, bf16[2,384,768]{2,1,0:T(8,128)(2,1)}, u32[]{:S(2)}) copy-start(bf16[2,384,768]{2,1,0:T(8,128)(2,1)} %param.7) | copy-start | bytes 3538948
  48.4 54.9 %all-to-all-start = ((bf16[32,2,9216]{2,1,0:T(2,128)(2,1)}), bf16[32,2,9216]{2,1,0:T(2,128)(2,1)S(1)}, u32[]{:S(2)}, u32[]{:S(2)}) async-start(bf16[32,2,9216]{2,1,0:T(2,128)(2,1)} %reshape.79), calls=%async_computation | async-start | bytes 2359296 | tf_op jit(solution)/shard_map/all_to_all | solution.py:43
  104.2 21.1 %copy-start.2 = (bf16[1,96,384]{2,1,0:T(8,128)(2,1)S(1)}, bf16[1,96,384]{2,1,0:T(8,128)(2,1)}, u32[]{:S(2)}) copy-start(bf16[1,96,384]{2,1,0:T(8,128)(2,1)} %get-tuple-element.10) | copy-start | bytes 221188
  107.7 7.5 %collective-permute-start = (bf16[48,192]{1,0:T(8,128)(2,1)S(1)}, bf16[48,192]{1,0:T(8,128)(2,1)S(1)}, u32[]{:S(2)}, u32[]{:S(2)}) collective-permute-start(bf16[48,192]{1,0:T(8,128)(2,1)S(1)} %fusion.14), channel_id=1, source_target_pairs={{0,0},{4,32},{8,64},{12,96},{16,128},{20,160},{24,192},{28,224},{3... | collective-permute-start | bytes 55304 | tf_op jit(solution)/shard_map/ppermute | solution.py:53
  115.9 22.1 %all-to-all-start.1 = ((bf16[8,48,192]{2,1,0:T(8,128)(2,1)}), bf16[8,48,192]{2,1,0:T(8,128)(2,1)S(1)}, u32[]{:S(2)}, u32[]{:S(2)}) async-start(bf16[8,48,192]{2,1,0:T(8,128)(2,1)} %broadcast_in_dim.15), calls=%async_computation.1 | async-start | bytes 393216 | tf_op jit(solution)/shard_map/all_to_all | solution.py:11
  165.0 9.6 %all-to-all-start.5 = ((bf16[8,384,24]{1,2,0:T(8,128)(2,1)}), bf16[8,384,24]{1,2,0:T(8,128)(2,1)S(1)}, u32[]{:S(2)}, u32[]{:S(2)}) async-start(bf16[8,384,24]{1,2,0:T(8,128)(2,1)} %broadcast_in_dim.17), calls=%async_computation.5 | async-start | bytes 294912 | tf_op jit(solution)/shard_map/all_to_all | solution.py:11
  186.3 22.9 %all-to-all-start.4 = ((bf16[32,384,24]{1,2,0:T(8,128)(2,1)}), bf16[32,384,24]{1,2,0:T(8,128)(2,1)S(1)}, u32[]{:S(2)}, u32[]{:S(2)}) async-start(bf16[32,384,24]{1,2,0:T(8,128)(2,1)} %broadcast_in_dim.16), calls=%async_computation.4 | async-start | bytes 1179648 | tf_op jit(solution)/shard_map/all_to_all | solution.py:11
  210.1 23.0 %all-to-all-start.7 = ((bf16[32,384,24]{1,2,0:T(8,128)(2,1)}), bf16[32,384,24]{1,2,0:T(8,128)(2,1)S(1)}, u32[]{:S(2)}, u32[]{:S(2)}) async-start(bf16[32,384,24]{1,2,0:T(8,128)(2,1)} %broadcast_in_dim.19), calls=%async_computation.7 | async-start | bytes 1179648 | tf_op jit(solution)/shard_map/all_to_all | solution.py:11
Sparse Core Ops, SparseCore 0:
  9.9 103.3 all-gather.2

commit v4 on v1

--- a/solution.py
+++ b/solution.py
@@ -40,26 +40,24 @@
 def on_device(prior_solved, lower_prior, rhs, coupling, inverse_diag):
     share_width = rhs.shape[2] // lax.axis_size("col")
     share_start = lax.axis_index("col") * share_width
+    stacked = jnp.concatenate([inverse_diag, coupling[None]], axis=0)
+    whole_blocks = lax.all_gather(stacked, "col", axis=1, tiled=True)
     depth, blocks, rows = lower_prior.shape
     both_terms = local_product(lower_prior.reshape(depth, blocks * rows), prior_solved)
     both_terms = both_terms.reshape(blocks, rows, rhs.shape[2])
-    first_share = sum_at_owner(both_terms[0], "col", 1)
-    second_share = sum_at_owner(both_terms[1], "col", 1)
-    first_block = lax.all_gather(inverse_diag[0], "col", axis=0, tiled=True)
-    cross_block = lax.all_gather(coupling, "col", axis=0, tiled=True)
-    second_block = lax.all_gather(inverse_diag[1], "col", axis=0, tiled=True)
+    shares = sum_at_owner(both_terms, "col", 2)
     rhs_share = lax.dynamic_slice_in_dim(rhs, share_start, share_width, 2).astype(jnp.float32)
 
     def apply_share(left_block, vector_rows):
         full_vector = collect(vector_rows, "row", 0)
         return local_product(left_block, full_vector)
 
-    first_reduced = (rhs_share[0] - first_share).astype(jnp.bfloat16)
-    first_solved = apply_share(first_block, first_reduced).astype(jnp.bfloat16)
+    first_reduced = (rhs_share[0] - shares[0]).astype(jnp.bfloat16)
+    first_solved = apply_share(whole_blocks[0], first_reduced).astype(jnp.bfloat16)
     first_out = collect(first_solved, "col", 1)
-    cross_term = apply_share(cross_block, first_solved)
-    second_reduced = (rhs_share[1] - second_share - cross_term).astype(jnp.bfloat16)
-    second_solved = apply_share(second_block, second_reduced).astype(jnp.bfloat16)
+    cross_term = apply_share(whole_blocks[2], first_solved)
+    second_reduced = (rhs_share[1] - shares[1] - cross_term).astype(jnp.bfloat16)
+    second_solved = apply_share(whole_blocks[1], second_reduced).astype(jnp.bfloat16)
     second_out = collect(second_solved, "col", 1)
     return jnp.stack([first_out, second_out])
 

time: 291 us -> 210 us (0.72)
  waiting for transfers between devices: 189 us -> 93.8 us
  blocking collectives: 39.6 us -> 50.6 us
  starting transfers between devices: 27.2 us -> 18.2 us
  other arithmetic: 0.3 us -> 4.89 us
  local copies, waits for them, and re-layouts: 10.2 us -> 14.3 us
    all_gather x3 -> x1, waiting for transfers between devices: 140 us -> 11 us  [on_device(): whole_blocks = lax.all_gather(stacked, 'col', axis=1, tiled=True)]
    all_to_all x2 -> x1, waiting for transfers between devices: 43.2 us -> 66.1 us  [sum_at_owner(): lax.all_to_all(in_blocks(array, dim, length), axis, 0, 0, tiled=True)]
    all_to_all x2 -> x1, waiting for transfers between devices: 4.75 us -> 16.6 us  [sent_to_all(): return lax.all_to_all(copies, axis, split_axis=0, concat_axis=0, tiled=True)]
    all_to_all x3 -> x4, blocking collectives: 39.6 us -> 50.6 us  [sent_to_all(): return lax.all_to_all(copies, axis, split_axis=0, concat_axis=0, tiled=True)]
    all_to_all x2 -> x1, starting transfers between devices: 16.6 us -> 11.3 us  [sum_at_owner(): lax.all_to_all(in_blocks(array, dim, length), axis, 0, 0, tiled=True)]
    unnamed x8, local copies, waits for them, and re-layouts: 3.65 us -> 8.25 us
    all_to_all x2 -> x1, starting transfers between devices: 10.4 us -> 6.84 us  [sent_to_all(): return lax.all_to_all(copies, axis, split_axis=0, concat_axis=0, tiled=True)]
    slice x2 -> x0, local copies, waits for them, and re-layouts: 3.29 us -> none  [the longest x1 1.69 us: on_device(): second_block = lax.all_gather(inverse_diag[1], 'col', axis=0, tiled=True)]
  transfers between devices with their start and end apart: 7 -> 3, of which waited for: 6 -> 3; matrix products, arithmetic and copies ran while one was open for 6% -> 12% of each run, Pallas kernels for 0% -> 0%
where the time goes in v4:
time: 210 us; the launch traced here: 209 us
  waiting for transfers between devices  93.8 us (45%)
  blocking collectives  50.6 us (24%)
  starting transfers between devices  18.2 us (9%)
  local copies, waits for them, and re-layouts  14.3 us (7%)
  between operations  13.5 us (6%)
  matrix products  13.3 us (6%)
  other arithmetic  4.89 us (2%)
    all_to_all x1, waiting for transfers between devices, sum_at_owner(): lax.all_to_all(in_blocks(array, dim, length), axis, 0, 0, tiled=True)  66.1 us
    all_to_all x4, blocking collectives, sent_to_all(): return lax.all_to_all(copies, axis, split_axis=0, concat_axis=0, tiled=True)  50.6 us
    all_to_all x1, waiting for transfers between devices, sent_to_all(): return lax.all_to_all(copies, axis, split_axis=0, concat_axis=0, tiled=True)  16.6 us
    dot_general x4, matrix products, local_product(): lax.dot_general(left_block, right_rows, (((0,), (0,)), ((), ())), preferr...  13.3 us
    all_to_all x1, starting transfers between devices, sum_at_owner(): lax.all_to_all(in_blocks(array, dim, length), axis, 0, 0, tiled=True)  11.3 us
    all_gather x1, waiting for transfers between devices, on_device(): whole_blocks = lax.all_gather(stacked, 'col', axis=1, tiled=True)  11 us
    unnamed x8, local copies, waits for them, and re-layouts  8.25 us
    all_to_all x1, starting transfers between devices, sent_to_all(): return lax.all_to_all(copies, axis, split_axis=0, concat_axis=0, tiled=True)  6.84 us
  transfers between devices with their start and end apart: 3, of which 3 were waited for; matrix products, arithmetic and copies ran while one was open for 12% of the time, Pallas kernels for 0%

profile of v4, /device:TPU:8, one launch (start us, length us, event | category | flops | bytes accessed | tf_op | source)
XLA Modules:
  0.0 208.7 jit_solution(10514598030689367120)
XLA Ops:
  6.5 0.0 copy-start
  6.5 0.0 all-gather.2.cloned.1.call-start
  6.5 1.8 pad_maximum_fusion.1
  8.3 0.0 all-gather.2.cloned.1.call-update
  8.3 6.6 %copy.31 = bf16[2880,768]{0,1:T(8,128)(2,1)} copy(bf16[2880,768]{1,0:T(8,128)(2,1)} %param.5) | data formatting | bytes 8847360 | tf_op args[0]
  14.9 7.1 %fusion.8 = f32[32,2,384,24]{2,0,3,1:T(8,128)S(1)} fusion(bf16[32,24,2880]{2,1,0:T(8,128)(2,1)} %bitcast.61, bf16[2880,2,384]{2,1,0:T(2,128)(2,1)} %param.6), kind=kOutput, calls=%fused_computation.11 | convolution fusion | flops 3397386240 | bytes 11206656 | tf_op jit(solution)/shard_map/dot_general | solution.py:35
  22.0 2.8 %copy.34 = f32[32,2,384,24]{2,3,1,0:T(8,128)} copy(f32[32,2,384,24]{2,0,3,1:T(8,128)S(1)} %fusion.8) | data formatting | bytes 4718592 | tf_op jit(solution)/shard_map/transpose | solution.py:10
  24.8 11.3 %all-to-all-start = ((f32[32,2,384,24]{2,3,1,0:T(8,128)}), f32[32,2,384,24]{2,3,1,0:T(8,128)S(1)}, u32[]{:S(2)}, u32[]{:S(2)}) async-start(f32[32,2,384,24]{2,3,1,0:T(8,128)} %copy.34), calls=%async_computation | async-start | bytes 4718592 | tf_op jit(solution)/shard_map/all_to_all | solution.py:15
  36.2 0.0 copy-done
  36.2 0.8 constant_dynamic-slice_fusion
  37.0 1.6 copy.42
  38.6 1.4 convert_element_type.18
  40.0 66.1 %all-to-all-done = f32[32,2,384,24]{2,3,1,0:T(8,128)S(1)} async-done(((f32[32,2,384,24]{2,3,1,0:T(8,128)}), f32[32,2,384,24]{2,3,1,0:T(8,128)S(1)}, u32[]{:S(2)}, u32[]{:S(2)}) %all-to-all-start) | async-done | bytes 2359328 | tf_op jit(solution)/shard_map/all_to_all | solution.py:15
  106.2 0.8 reduce_sum.9
  106.9 0.0 copy-start.1
  106.9 0.8 fusion.19
  107.8 9.6 %all_to_all.30 = bf16[8,384,24]{1,2,0:T(8,128)(2,1)S(1)} all-to-all(bf16[8,384,24]{1,2,0:T(8,128)(2,1)S(1)} %broadcast_in_dim.19), channel_id=1, replica_groups=mesh['row'=8,'col'=32] {'row'}, dimensions={0} | all-to-all | bytes 294912 | tf_op jit(solution)/shard_map/all_to_all | solution.py:27
  117.4 11.0 %all-gather.2.cloned.1.call-done = bf16[3,3072,384]{2,1,0:T(8,128)(2,1)} async-done(((bf16[3,96,384]{2,1,0:T(8,128)(2,1)}), bf16[3,3072,384]{2,1,0:T(8,128)(2,1)}) %all-gather.2.cloned.1.call-update) | async-done | bytes 7077904 | tf_op jit(solution)/shard_map/all_gather | solution.py:44
  128.4 2.1 fusion.15
  130.5 9.5 %all_to_all.31 = bf16[8,384,24]{1,2,0:T(8,128)(2,1)S(1)} all-to-all(bf16[8,384,24]{1,2,0:T(8,128)(2,1)S(1)} %broadcast_in_dim.21), channel_id=1, replica_groups=mesh['row'=8,'col'=32] {'row'}, dimensions={0} | all-to-all | bytes 294912 | tf_op jit(solution)/shard_map/all_to_all | solution.py:27
  140.1 0.0 copy-done.1
  140.1 0.0 copy-done.2
  140.1 2.1 %fusion.14 = bf16[384,24]{0,1:T(8,128)(2,1)S(1)} fusion(bf16[3072,24]{0,1:T(8,128)(2,1)S(1)} %bitcast.68, bf16[3,3072,384]{2,1,0:T(8,128)(2,1)} %all-gather.2.cloned.1.call-done, f32[2,384,24]{1,2,0:T(8,128)S(1)} %copy-done.2, f32[2,384,24]{1,2,0:T(8,128)S(1)} %copy-done.1), kind=kOutput, calls=%fused_computation.14 | convolution fusion | flops 56650752 | bytes 2598912 | tf_op jit(solution)/shard_map/dot_general | solution.py:35
  142.2 8.7 %all_to_all.32 = bf16[8,384,24]{1,2,0:T(8,128)(2,1)S(1)} all-to-all(bf16[8,384,24]{1,2,0:T(8,128)(2,1)S(1)} %broadcast_in_dim.22), channel_id=1, replica_groups=mesh['row'=8,'col'=32] {'row'}, dimensions={0} | all-to-all | bytes 294912 | tf_op jit(solution)/shard_map/all_to_all | solution.py:27
  150.9 0.9 broadcast_in_dim.20
  151.8 6.8 %all-to-all-start.2 = ((bf16[32,384,24]{1,2,0:T(8,128)(2,1)}), bf16[32,384,24]{1,2,0:T(8,128)(2,1)S(1)}, u32[]{:S(2)}, u32[]{:S(2)}) async-start(bf16[32,384,24]{1,2,0:T(8,128)(2,1)} %broadcast_in_dim.20), calls=%async_computation.2 | async-start | bytes 1179648 | tf_op jit(solution)/shard_map/all_to_all | solution.py:27
  158.6 2.1 fusion.16
  160.7 16.6 %all-to-all-done.2 = bf16[32,384,24]{1,2,0:T(8,128)(2,1)S(1)} async-done(((bf16[32,384,24]{1,2,0:T(8,128)(2,1)}), bf16[32,384,24]{1,2,0:T(8,128)(2,1)S(1)}, u32[]{:S(2)}, u32[]{:S(2)}) %all-to-all-start.2) | async-done | bytes 589856 | tf_op jit(solution)/shard_map/all_to_all | solution.py:27
  177.4 0.1 broadcast_in_dim.23
  177.4 22.8 %all_to_all.33 = bf16[32,384,24]{1,2,0:T(8,128)(2,1)S(1)} all-to-all(bf16[32,384,24]{1,2,0:T(8,128)(2,1)S(1)} %broadcast_in_dim.23), channel_id=1, replica_groups=mesh['row'=8,'col'=32] {'col'}, dimensions={0} | all-to-all | bytes 1179648 | tf_op jit(solution)/shard_map/all_to_all | solution.py:27
  200.2 0.1 pad_maximum_fusion
  200.4 1.5 copy.38
  (7 shorter events, 0.1 us)
Async XLA Ops:
  6.5 29.6 %copy-start = (bf16[2,384,768]{2,1,0:T(8,128)(2,1)S(1)}, bf16[2,384,768]{2,1,0:T(8,128)(2,1)}, u32[]{:S(2)}) copy-start(bf16[2,384,768]{2,1,0:T(8,128)(2,1)} %param.7) | copy-start | bytes 3538948
  6.5 121.9 %all-gather.2.cloned.1.call-start = ((), (), s32[]{:S(2)}) async-start(), calls=%async_computation.6 | async-start | bytes 7299072 | tf_op jit(solution)/shard_map/all_gather | solution.py:44
  24.8 81.3 %all-to-all-start = ((f32[32,2,384,24]{2,3,1,0:T(8,128)}), f32[32,2,384,24]{2,3,1,0:T(8,128)S(1)}, u32[]{:S(2)}, u32[]{:S(2)}) async-start(f32[32,2,384,24]{2,3,1,0:T(8,128)} %copy.34), calls=%async_computation | async-start | bytes 4718592 | tf_op jit(solution)/shard_map/all_to_all | solution.py:15
  106.9 33.2 %copy-start.1 = (f32[2,384,24]{1,2,0:T(8,128)S(1)}, f32[2,384,24]{1,2,0:T(8,128)}, u32[]{:S(2)}) copy-start(f32[2,384,24]{1,2,0:T(8,128)} %convert_element_type.18) | copy-start | bytes 221188
  106.9 33.2 %copy-start.2 = (f32[2,384,24]{1,2,0:T(8,128)S(1)}, f32[2,384,24]{1,2,0:T(8,128)}, u32[]{:S(2)}) copy-start(f32[2,384,24]{1,2,0:T(8,128)} %reduce_sum.9) | copy-start | bytes 221188
  151.8 25.6 %all-to-all-start.2 = ((bf16[32,384,24]{1,2,0:T(8,128)(2,1)}), bf16[32,384,24]{1,2,0:T(8,128)(2,1)S(1)}, u32[]{:S(2)}, u32[]{:S(2)}) async-start(bf16[32,384,24]{1,2,0:T(8,128)(2,1)} %broadcast_in_dim.20), calls=%async_computation.2 | async-start | bytes 1179648 | tf_op jit(solution)/shard_map/all_to_all | solution.py:27
Sparse Core Ops, SparseCore 0:
  9.9 118.4 all-gather.1

commit v5 on v4

--- a/solution.py
+++ b/solution.py
@@ -54,12 +54,11 @@
 
     first_reduced = (rhs_share[0] - shares[0]).astype(jnp.bfloat16)
     first_solved = apply_share(whole_blocks[0], first_reduced).astype(jnp.bfloat16)
-    first_out = collect(first_solved, "col", 1)
     cross_term = apply_share(whole_blocks[2], first_solved)
     second_reduced = (rhs_share[1] - shares[1] - cross_term).astype(jnp.bfloat16)
     second_solved = apply_share(whole_blocks[1], second_reduced).astype(jnp.bfloat16)
-    second_out = collect(second_solved, "col", 1)
-    return jnp.stack([first_out, second_out])
+    solved_share = jnp.stack([first_solved, second_solved])
+    return collect(solved_share, "col", 2)
 
 
 def solution(mesh):

time: 210 us -> 202 us (0.962)
  waiting for transfers between devices: 93.8 us -> 77.2 us
  blocking collectives: 50.6 us -> 67.1 us
  starting transfers between devices: 18.2 us -> 11.3 us
    all_to_all x1 -> x0, waiting for transfers between devices: 16.6 us -> none  [sent_to_all(): return lax.all_to_all(copies, axis, split_axis=0, concat_axis=0, tiled=True)]
    all_to_all x4, blocking collectives: 50.6 us -> 67.1 us  [sent_to_all(): return lax.all_to_all(copies, axis, split_axis=0, concat_axis=0, tiled=True)]
    all_to_all x1 -> x0, starting transfers between devices: 6.84 us -> none  [sent_to_all(): return lax.all_to_all(copies, axis, split_axis=0, concat_axis=0, tiled=True)]
  transfers between devices with their start and end apart: 3 -> 2, of which waited for: 3 -> 2; matrix products, arithmetic and copies ran while one was open for 12% -> 11% of each run, Pallas kernels for 0% -> 0%
where the time goes in v5:
time: 202 us; the launch traced here: 201 us
  waiting for transfers between devices  77.2 us (38%)
  blocking collectives  67.1 us (33%)
  local copies, waits for them, and re-layouts  13.7 us (7%)
  between operations  13.5 us (7%)
  matrix products  13.3 us (7%)
  starting transfers between devices  11.3 us (6%)
  other arithmetic  4.75 us (2%)
    all_to_all x4, blocking collectives, sent_to_all(): return lax.all_to_all(copies, axis, split_axis=0, concat_axis=0, tiled=True)  67.1 us
    all_to_all x1, waiting for transfers between devices, sum_at_owner(): lax.all_to_all(in_blocks(array, dim, length), axis, 0, 0, tiled=True)  66.1 us
    dot_general x4, matrix products, local_product(): lax.dot_general(left_block, right_rows, (((0,), (0,)), ((), ())), preferr...  13.3 us
    all_to_all x1, starting transfers between devices, sum_at_owner(): lax.all_to_all(in_blocks(array, dim, length), axis, 0, 0, tiled=True)  11.3 us
    all_gather x1, waiting for transfers between devices, on_device(): whole_blocks = lax.all_gather(stacked, 'col', axis=1, tiled=True)  11.1 us
    unnamed x8, local copies, waits for them, and re-layouts  8.29 us
  transfers between devices with their start and end apart: 2, of which 2 were waited for; matrix products, arithmetic and copies ran while one was open for 11% of the time, Pallas kernels for 0%

profile of v5, /device:TPU:8, one launch (start us, length us, event | category | flops | bytes accessed | tf_op | source)
XLA Modules:
  0.0 200.9 jit_solution(5626200719113295924)
XLA Ops:
  6.5 0.0 copy-start
  6.5 0.0 all-gather.2.cloned.1.call-start
  6.5 1.8 pad_maximum_fusion
  8.3 0.0 all-gather.2.cloned.1.call-update
  8.3 6.6 %copy.31 = bf16[2880,768]{0,1:T(8,128)(2,1)} copy(bf16[2880,768]{1,0:T(8,128)(2,1)} %param.5) | data formatting | bytes 8847360 | tf_op args[0]
  14.9 7.1 %fusion.8 = f32[32,2,384,24]{2,0,3,1:T(8,128)S(1)} fusion(bf16[32,24,2880]{2,1,0:T(8,128)(2,1)} %bitcast.64, bf16[2880,2,384]{2,1,0:T(2,128)(2,1)} %param.6), kind=kOutput, calls=%fused_computation.11 | convolution fusion | flops 3397386240 | bytes 11206656 | tf_op jit(solution)/shard_map/dot_general | solution.py:35
  22.0 2.8 %copy.34 = f32[32,2,384,24]{2,3,1,0:T(8,128)} copy(f32[32,2,384,24]{2,0,3,1:T(8,128)S(1)} %fusion.8) | data formatting | bytes 4718592 | tf_op jit(solution)/shard_map/transpose | solution.py:10
  24.9 11.3 %all-to-all-start = ((f32[32,2,384,24]{2,3,1,0:T(8,128)}), f32[32,2,384,24]{2,3,1,0:T(8,128)S(1)}, u32[]{:S(2)}, u32[]{:S(2)}) async-start(f32[32,2,384,24]{2,3,1,0:T(8,128)} %copy.34), calls=%async_computation | async-start | bytes 4718592 | tf_op jit(solution)/shard_map/all_to_all | solution.py:15
  36.2 0.0 copy-done
  36.2 0.8 constant_dynamic-slice_fusion
  37.0 1.7 copy.43
  38.7 1.4 convert_element_type.18
  40.1 66.1 %all-to-all-done = f32[32,2,384,24]{2,3,1,0:T(8,128)S(1)} async-done(((f32[32,2,384,24]{2,3,1,0:T(8,128)}), f32[32,2,384,24]{2,3,1,0:T(8,128)S(1)}, u32[]{:S(2)}, u32[]{:S(2)}) %all-to-all-start) | async-done | bytes 2359328 | tf_op jit(solution)/shard_map/all_to_all | solution.py:15
  106.2 0.7 reduce_sum.9
  106.9 0.0 copy-start.1
  106.9 0.0 copy-start.2
  106.9 0.8 fusion.20
  107.8 9.6 %all_to_all.25 = bf16[8,384,24]{1,2,0:T(8,128)(2,1)S(1)} all-to-all(bf16[8,384,24]{1,2,0:T(8,128)(2,1)S(1)} %broadcast_in_dim.16), channel_id=1, replica_groups=mesh['row'=8,'col'=32] {'row'}, dimensions={0} | all-to-all | bytes 294912 | tf_op jit(solution)/shard_map/all_to_all | solution.py:27
  117.4 11.1 %all-gather.2.cloned.1.call-done = bf16[3,3072,384]{2,1,0:T(8,128)(2,1)} async-done(((bf16[3,96,384]{2,1,0:T(8,128)(2,1)}), bf16[3,3072,384]{2,1,0:T(8,128)(2,1)}) %all-gather.2.cloned.1.call-update) | async-done | bytes 7077904 | tf_op jit(solution)/shard_map/all_gather | solution.py:44
  128.4 2.1 %fusion.15 = bf16[384,24]{0,1:T(8,128)(2,1)S(1)} fusion(bf16[3072,24]{0,1:T(8,128)(2,1)S(1)} %bitcast.68, bf16[3,3072,384]{2,1,0:T(8,128)(2,1)} %all-gather.2.cloned.1.call-done), kind=kOutput, calls=%fused_computation.14 | convolution fusion | flops 56632320 | bytes 2525184 | tf_op jit(solution)/shard_map/dot_general | solution.py:35
  130.6 9.5 %all_to_all.26 = bf16[8,384,24]{1,2,0:T(8,128)(2,1)S(1)} all-to-all(bf16[8,384,24]{1,2,0:T(8,128)(2,1)S(1)} %broadcast_in_dim.17), channel_id=1, replica_groups=mesh['row'=8,'col'=32] {'row'}, dimensions={0} | all-to-all | bytes 294912 | tf_op jit(solution)/shard_map/all_to_all | solution.py:27
  140.1 0.0 copy-done.1
  140.1 0.0 copy-done.2
  140.1 2.1 %fusion.14 = bf16[384,24]{0,1:T(8,128)(2,1)S(1)} fusion(bf16[3072,24]{0,1:T(8,128)(2,1)S(1)} %bitcast.69, bf16[3,3072,384]{2,1,0:T(8,128)(2,1)} %all-gather.2.cloned.1.call-done, f32[2,384,24]{1,2,0:T(8,128)S(1)} %copy-done.2, f32[2,384,24]{1,2,0:T(8,128)S(1)} %copy-done.1), kind=kOutput, calls=%fused_computation.13 | convolution fusion | flops 56650752 | bytes 2598912 | tf_op jit(solution)/shard_map/dot_general | solution.py:35
  142.3 8.7 %all_to_all.27 = bf16[8,384,24]{1,2,0:T(8,128)(2,1)S(1)} all-to-all(bf16[8,384,24]{1,2,0:T(8,128)(2,1)S(1)} %broadcast_in_dim.18), channel_id=1, replica_groups=mesh['row'=8,'col'=32] {'row'}, dimensions={0} | all-to-all | bytes 294912 | tf_op jit(solution)/shard_map/all_to_all | solution.py:27
  150.9 2.1 %fusion.17 = bf16[1,384,24]{1,2,0:T(8,128)(2,1)S(1)} fusion(bf16[3072,24]{0,1:T(8,128)(2,1)S(1)} %bitcast.70, bf16[3,3072,384]{2,1,0:T(8,128)(2,1)} %all-gather.2.cloned.1.call-done), kind=kOutput, calls=%fused_computation.16 | convolution fusion | flops 56632320 | bytes 2525184 | tf_op jit(solution)/shard_map/dot_general | solution.py:35
  153.0 0.1 broadcast_in_dim.19
  153.2 39.4 %all_to_all.28 = bf16[32,2,384,24]{2,3,1,0:T(8,128)(2,1)S(1)} all-to-all(bf16[32,2,384,24]{2,3,1,0:T(8,128)(2,1)S(1)} %broadcast_in_dim.19), channel_id=1, replica_groups=mesh['row'=8,'col'=32] {'col'}, dimensions={0} | all-to-all | bytes 2359296 | tf_op jit(solution)/shard_map/all_to_all | solution.py:27
  192.5 0.1 copy.38
  192.6 1.5 copy.39
  (7 shorter events, 0.1 us)
Async XLA Ops:
  6.5 29.7 %copy-start = (bf16[2,384,768]{2,1,0:T(8,128)(2,1)S(1)}, bf16[2,384,768]{2,1,0:T(8,128)(2,1)}, u32[]{:S(2)}) copy-start(bf16[2,384,768]{2,1,0:T(8,128)(2,1)} %param.7) | copy-start | bytes 3538948
  6.5 121.9 %all-gather.2.cloned.1.call-start = ((), (), s32[]{:S(2)}) async-start(), calls=%async_computation.5 | async-start | bytes 7299072 | tf_op jit(solution)/shard_map/all_gather | solution.py:44
  24.9 81.3 %all-to-all-start = ((f32[32,2,384,24]{2,3,1,0:T(8,128)}), f32[32,2,384,24]{2,3,1,0:T(8,128)S(1)}, u32[]{:S(2)}, u32[]{:S(2)}) async-start(f32[32,2,384,24]{2,3,1,0:T(8,128)} %copy.34), calls=%async_computation | async-start | bytes 4718592 | tf_op jit(solution)/shard_map/all_to_all | solution.py:15
  106.9 33.2 %copy-start.1 = (f32[2,384,24]{1,2,0:T(8,128)S(1)}, f32[2,384,24]{1,2,0:T(8,128)}, u32[]{:S(2)}) copy-start(f32[2,384,24]{1,2,0:T(8,128)} %convert_element_type.18) | copy-start | bytes 221188
  106.9 33.2 %copy-start.2 = (f32[2,384,24]{1,2,0:T(8,128)S(1)}, f32[2,384,24]{1,2,0:T(8,128)}, u32[]{:S(2)}) copy-start(f32[2,384,24]{1,2,0:T(8,128)} %reduce_sum.9) | copy-start | bytes 221188
Sparse Core Ops, SparseCore 0:
  9.9 118.4 all-gather.1

commit v6 on v5

--- a/solution.py
+++ b/solution.py
@@ -28,7 +28,9 @@
 
 
 def collect(array, axis, dim):
-    return in_order(sent_to_all(array, axis), dim)
+    flat = array.reshape(array.size // 128, 128)
+    got = sent_to_all(flat, axis).reshape(lax.axis_size(axis), *array.shape)
+    return in_order(got, dim)
 
 
 def local_product(left_block, right_rows):

time: 202 us -> 220 us (1.089)
  local copies, waits for them, and re-layouts: 13.7 us -> 32.8 us
    reshape x0 -> x4, local copies, waits for them, and re-layouts: none -> 10.1 us  [the longest x1 9.54 us: collect(): got = sent_to_all(flat, axis).reshape(lax.axis_size(axis), *array.shape)]
    transpose x0 -> x1, local copies, waits for them, and re-layouts: none -> 5.21 us  [in_order(): blocks = jnp.moveaxis(blocks, 0, dim)]
    another operation x0 -> x4, local copies, waits for them, and re-layouts: none -> 3.32 us  [the longest x3 3.15 us: in_order(): blocks.reshape(*dims[:dim], dims[dim] * dims[dim + 1], *dims[dim + 2:])]
where the time goes in v6:
time: 220 us; the launch traced here: 219 us
  waiting for transfers between devices  75.9 us (35%)
  blocking collectives  67.1 us (30%)
  local copies, waits for them, and re-layouts  32.8 us (15%)
  between operations  13.6 us (6%)
  matrix products  13.5 us (6%)
  starting transfers between devices  11.3 us (5%)
  other arithmetic  4.75 us (2%)
    all_to_all x4, blocking collectives, sent_to_all(): return lax.all_to_all(copies, axis, split_axis=0, concat_axis=0, tiled=True)  67.1 us
    all_to_all x1, waiting for transfers between devices, sum_at_owner(): lax.all_to_all(in_blocks(array, dim, length), axis, 0, 0, tiled=True)  66.1 us
    dot_general x4, matrix products, local_product(): lax.dot_general(left_block, right_rows, (((0,), (0,)), ((), ())), preferr...  13.5 us
    all_to_all x1, starting transfers between devices, sum_at_owner(): lax.all_to_all(in_blocks(array, dim, length), axis, 0, 0, tiled=True)  11.3 us
    all_gather x1, waiting for transfers between devices, on_device(): whole_blocks = lax.all_gather(stacked, 'col', axis=1, tiled=True)  9.74 us
    reshape x1, local copies, waits for them, and re-layouts, collect(): got = sent_to_all(flat, axis).reshape(lax.axis_size(axis), *array.shape)  9.54 us
    unnamed x8, local copies, waits for them, and re-layouts  8.29 us
    transpose x1, local copies, waits for them, and re-layouts, in_order(): blocks = jnp.moveaxis(blocks, 0, dim)  5.21 us
  transfers between devices with their start and end apart: 2, of which 2 were waited for; matrix products, arithmetic and copies ran while one was open for 11% of the time, Pallas kernels for 0%

profile of v6, /device:TPU:8, one launch (start us, length us, event | category | flops | bytes accessed | tf_op | source)
XLA Modules:
  0.0 218.9 jit_solution(10874083391221959744)
XLA Ops:
  6.5 1.8 pad_maximum_fusion
  8.3 6.6 %copy.21 = bf16[2880,768]{0,1:T(8,128)(2,1)} copy(bf16[2880,768]{1,0:T(8,128)(2,1)} %param.5) | data formatting | bytes 8847360 | tf_op args[0]
  14.9 7.1 %fusion.8 = f32[32,2,384,24]{2,0,3,1:T(8,128)S(1)} fusion(bf16[32,24,2880]{2,1,0:T(8,128)(2,1)} %bitcast.56, bf16[2880,2,384]{2,1,0:T(2,128)(2,1)} %param.6), kind=kOutput, calls=%fused_computation.11 | convolution fusion | flops 3397386240 | bytes 11206656 | tf_op jit(solution)/shard_map/dot_general | solution.py:37
  22.0 2.8 %copy.24 = f32[32,2,384,24]{2,3,1,0:T(8,128)} copy(f32[32,2,384,24]{2,0,3,1:T(8,128)S(1)} %fusion.8) | data formatting | bytes 4718592 | tf_op jit(solution)/shard_map/transpose | solution.py:10
  24.9 11.3 %all-to-all-start = ((f32[32,2,384,24]{2,3,1,0:T(8,128)}), f32[32,2,384,24]{2,3,1,0:T(8,128)S(1)}, u32[]{:S(2)}, u32[]{:S(2)}) async-start(f32[32,2,384,24]{2,3,1,0:T(8,128)} %copy.24), calls=%async_computation | async-start | bytes 4718592 | tf_op jit(solution)/shard_map/all_to_all | solution.py:15
  36.2 0.8 constant_dynamic-slice_fusion
  37.0 1.7 copy.34
  38.7 1.4 convert_element_type.19
  40.1 66.1 %all-to-all-done = f32[32,2,384,24]{2,3,1,0:T(8,128)S(1)} async-done(((f32[32,2,384,24]{2,3,1,0:T(8,128)}), f32[32,2,384,24]{2,3,1,0:T(8,128)S(1)}, u32[]{:S(2)}, u32[]{:S(2)}) %all-to-all-start) | async-done | bytes 2359328 | tf_op jit(solution)/shard_map/all_to_all | solution.py:15
  106.2 0.7 reduce_sum.9
  106.9 0.8 fusion.19
  107.8 0.1 copy.25
  107.9 0.2 convert_element_type.21
  108.1 9.6 %all_to_all.25 = bf16[8,72,128]{2,1,0:T(8,128)(2,1)S(1)} all-to-all(bf16[8,72,128]{2,1,0:T(8,128)(2,1)S(1)} %broadcast_in_dim.16), channel_id=1, replica_groups=mesh['row'=8,'col'=32] {'row'}, dimensions={0} | all-to-all | bytes 294912 | tf_op jit(solution)/shard_map/all_to_all | solution.py:27
  117.6 1.1 reshape_reshape.10
  118.7 9.7 %all-gather.2.cloned.1.call-done = bf16[3,3072,384]{2,1,0:T(8,128)(2,1)} async-done(((bf16[3,96,384]{2,1,0:T(8,128)(2,1)}), bf16[3,3072,384]{2,1,0:T(8,128)(2,1)}) %all-gather.2.cloned.1.call-update) | async-done | bytes 7077904 | tf_op jit(solution)/shard_map/all_gather | solution.py:46
  128.4 2.1 fusion.15
  130.7 0.2 reshape.27
  130.9 9.5 %all_to_all.26 = bf16[8,72,128]{2,1,0:T(8,128)(2,1)S(1)} all-to-all(bf16[8,72,128]{2,1,0:T(8,128)(2,1)S(1)} %broadcast_in_dim.17), channel_id=1, replica_groups=mesh['row'=8,'col'=32] {'row'}, dimensions={0} | all-to-all | bytes 294912 | tf_op jit(solution)/shard_map/all_to_all | solution.py:27
  140.4 1.1 reshape_reshape.11
  141.5 2.1 fusion.14
  143.8 0.2 reshape.28
  144.0 8.7 %all_to_all.27 = bf16[8,72,128]{2,1,0:T(8,128)(2,1)S(1)} all-to-all(bf16[8,72,128]{2,1,0:T(8,128)(2,1)S(1)} %broadcast_in_dim.18), channel_id=1, replica_groups=mesh['row'=8,'col'=32] {'row'}, dimensions={0} | all-to-all | bytes 294912 | tf_op jit(solution)/shard_map/all_to_all | solution.py:27
  152.6 1.1 reshape_reshape.12
  153.7 2.1 fusion.17
  155.8 0.2 copy.28
  156.0 0.3 reshape.29
  156.3 0.2 broadcast_in_dim.19
  156.4 39.4 %all_to_all.28 = bf16[32,144,128]{2,1,0:T(8,128)(2,1)S(1)} all-to-all(bf16[32,144,128]{2,1,0:T(8,128)(2,1)S(1)} %broadcast_in_dim.19), channel_id=1, replica_groups=mesh['row'=8,'col'=32] {'col'}, dimensions={0} | all-to-all | bytes 2359296 | tf_op jit(solution)/shard_map/all_to_all | solution.py:27
  195.8 9.5 %reshape.30 = bf16[32,2,384,24]{3,2,1,0:T(8,128)(2,1)} reshape(bf16[32,144,128]{2,1,0:T(8,128)(2,1)S(1)} %all_to_all.28) | data formatting | bytes 2359296 | tf_op jit(solution)/shard_map/reshape | solution.py:32
  205.3 5.2 %copy.29 = bf16[2,384,32,24]{1,3,2,0:T(8,128)(2,1)S(1)} copy(bf16[2,384,32,24]{3,1,0,2:T(8,128)(2,1)} %bitcast.54) | data formatting | bytes 2359296 | tf_op jit(solution)/shard_map/transpose | solution.py:20
  210.6 1.5 copy.30
  (14 shorter events, 0.4 us)
Async XLA Ops:
  6.5 29.7 %copy-start = (bf16[2,384,768]{2,1,0:T(8,128)(2,1)S(1)}, bf16[2,384,768]{2,1,0:T(8,128)(2,1)}, u32[]{:S(2)}) copy-start(bf16[2,384,768]{2,1,0:T(8,128)(2,1)} %param.7) | copy-start | bytes 3538948
  6.5 121.9 %all-gather.2.cloned.1.call-start = ((), (), s32[]{:S(2)}) async-start(), calls=%async_computation.5 | async-start | bytes 7299072 | tf_op jit(solution)/shard_map/all_gather | solution.py:46
  24.9 81.3 %all-to-all-start = ((f32[32,2,384,24]{2,3,1,0:T(8,128)}), f32[32,2,384,24]{2,3,1,0:T(8,128)S(1)}, u32[]{:S(2)}, u32[]{:S(2)}) async-start(f32[32,2,384,24]{2,3,1,0:T(8,128)} %copy.24), calls=%async_computation | async-start | bytes 4718592 | tf_op jit(solution)/shard_map/all_to_all | solution.py:15
  106.9 34.6 %copy-start.1 = (f32[2,384,24]{1,2,0:T(8,128)S(1)}, f32[2,384,24]{1,2,0:T(8,128)}, u32[]{:S(2)}) copy-start(f32[2,384,24]{1,2,0:T(8,128)} %convert_element_type.19) | copy-start | bytes 221188
  106.9 34.6 %copy-start.2 = (f32[2,384,24]{1,2,0:T(8,128)S(1)}, f32[2,384,24]{1,2,0:T(8,128)}, u32[]{:S(2)}) copy-start(f32[2,384,24]{1,2,0:T(8,128)} %reduce_sum.9) | copy-start | bytes 221188
Sparse Core Ops, SparseCore 0:
  9.9 118.4 all-gather.1

commit v7 on v5

--- a/solution.py
+++ b/solution.py
@@ -1,7 +1,9 @@
 import jax
 import jax.numpy as jnp
 from jax import lax
-from jax.sharding import PartitionSpec as P
+from jax.sharding import Mesh, PartitionSpec as P
+
+COL = ("z", "x")
 
 
 def in_blocks(array, dim, length):
@@ -38,14 +40,14 @@
 
 
 def on_device(prior_solved, lower_prior, rhs, coupling, inverse_diag):
-    share_width = rhs.shape[2] // lax.axis_size("col")
-    share_start = lax.axis_index("col") * share_width
+    share_width = rhs.shape[2] // lax.axis_size(COL)
+    share_start = lax.axis_index(COL) * share_width
     stacked = jnp.concatenate([inverse_diag, coupling[None]], axis=0)
-    whole_blocks = lax.all_gather(stacked, "col", axis=1, tiled=True)
+    whole_blocks = lax.all_gather(stacked, COL, axis=1, tiled=True)
     depth, blocks, rows = lower_prior.shape
     both_terms = local_product(lower_prior.reshape(depth, blocks * rows), prior_solved)
     both_terms = both_terms.reshape(blocks, rows, rhs.shape[2])
-    shares = sum_at_owner(both_terms, "col", 2)
+    shares = sum_at_owner(both_terms, COL, 2)
     rhs_share = lax.dynamic_slice_in_dim(rhs, share_start, share_width, 2).astype(jnp.float32)
 
     def apply_share(left_block, vector_rows):
@@ -58,19 +60,22 @@
     second_reduced = (rhs_share[1] - shares[1] - cross_term).astype(jnp.bfloat16)
     second_solved = apply_share(whole_blocks[1], second_reduced).astype(jnp.bfloat16)
     solved_share = jnp.stack([first_solved, second_solved])
-    return collect(solved_share, "col", 2)
+    across_x = lax.all_gather(solved_share, "x", axis=2, tiled=True)
+    return collect(across_x, "z", 2)
 
 
 def solution(mesh):
+    nrow, ncol = mesh.devices.shape
+    fine = Mesh(mesh.devices.reshape(nrow, nrow, ncol // nrow), ("row", "z", "x"))
     return jax.shard_map(
         on_device,
-        mesh=mesh,
+        mesh=fine,
         in_specs=(
-            P("col", None),
-            P("col", None, "row"),
+            P(COL, None),
+            P(COL, None, "row"),
             P(None, "row", None),
-            P("col", "row"),
-            P(None, "col", "row"),
+            P(COL, "row"),
+            P(None, COL, "row"),
         ),
         out_specs=P(None, "row", None),
         check_vma=False,

time: 202 us -> 208 us (1.030)
  blocking collectives: 67.1 us -> 73.5 us
    all_gather x0 -> x1, blocking collectives: none -> 12.1 us  [on_device(): across_x = lax.all_gather(solved_share, 'x', axis=2, tiled=True)]
    all_to_all x4, blocking collectives: 67.1 us -> 61.5 us  [sent_to_all(): return lax.all_to_all(copies, axis, split_axis=0, concat_axis=0, tiled=True)]
where the time goes in v7:
time: 208 us; the launch traced here: 207 us
  waiting for transfers between devices  77.2 us (37%)
  blocking collectives  73.5 us (35%)
  local copies, waits for them, and re-layouts  13.7 us (7%)
  between operations  13.5 us (6%)
  matrix products  13.3 us (6%)
  starting transfers between devices  11.3 us (5%)
  other arithmetic  4.75 us (2%)
    all_to_all x1, waiting for transfers between devices, sum_at_owner(): lax.all_to_all(in_blocks(array, dim, length), axis, 0, 0, tiled=True)  66.1 us
    all_to_all x4, blocking collectives, sent_to_all(): return lax.all_to_all(copies, axis, split_axis=0, concat_axis=0, tiled=True)  61.5 us
    dot_general x4, matrix products, local_product(): lax.dot_general(left_block, right_rows, (((0,), (0,)), ((), ())), preferr...  13.3 us
    all_gather x1, blocking collectives, on_device(): across_x = lax.all_gather(solved_share, 'x', axis=2, tiled=True)  12.1 us
    all_to_all x1, starting transfers between devices, sum_at_owner(): lax.all_to_all(in_blocks(array, dim, length), axis, 0, 0, tiled=True)  11.3 us
    all_gather x1, waiting for transfers between devices, on_device(): whole_blocks = lax.all_gather(stacked, COL, axis=1, tiled=True)  11.1 us
    unnamed x8, local copies, waits for them, and re-layouts  8.29 us
  transfers between devices with their start and end apart: 2, of which 2 were waited for; matrix products, arithmetic and copies ran while one was open for 11% of the time, Pallas kernels for 0%

profile of v7, /device:TPU:8, one launch (start us, length us, event | category | flops | bytes accessed | tf_op | source)
XLA Modules:
  0.0 207.4 jit_solution(7967077803670387101)
XLA Ops:
  6.5 0.0 copy-start
  6.5 0.0 all-gather.2.cloned.1.call-start
  6.5 1.8 pad_maximum_fusion
  8.3 0.0 all-gather.2.cloned.1.call-update
  8.3 6.6 %copy.31 = bf16[2880,768]{0,1:T(8,128)(2,1)} copy(bf16[2880,768]{1,0:T(8,128)(2,1)} %param.5) | data formatting | bytes 8847360 | tf_op args[0]
  14.9 7.1 %fusion.8 = f32[32,2,384,24]{2,0,3,1:T(8,128)S(1)} fusion(bf16[32,24,2880]{2,1,0:T(8,128)(2,1)} %bitcast.64, bf16[2880,2,384]{2,1,0:T(2,128)(2,1)} %param.6), kind=kOutput, calls=%fused_computation.11 | convolution fusion | flops 3397386240 | bytes 11206656 | tf_op jit(solution)/shard_map/dot_general | solution.py:37
  22.0 2.8 %copy.34 = f32[32,2,384,24]{2,3,1,0:T(8,128)} copy(f32[32,2,384,24]{2,0,3,1:T(8,128)S(1)} %fusion.8) | data formatting | bytes 4718592 | tf_op jit(solution)/shard_map/transpose | solution.py:12
  24.9 11.3 %all-to-all-start = ((f32[32,2,384,24]{2,3,1,0:T(8,128)}), f32[32,2,384,24]{2,3,1,0:T(8,128)S(1)}, u32[]{:S(2)}, u32[]{:S(2)}) async-start(f32[32,2,384,24]{2,3,1,0:T(8,128)} %copy.34), calls=%async_computation | async-start | bytes 4718592 | tf_op jit(solution)/shard_map/all_to_all | solution.py:17
  36.2 0.0 copy-done
  36.2 0.8 constant_dynamic-slice_fusion
  37.0 1.7 copy.43
  38.7 1.4 convert_element_type.18
  40.1 66.1 %all-to-all-done = f32[32,2,384,24]{2,3,1,0:T(8,128)S(1)} async-done(((f32[32,2,384,24]{2,3,1,0:T(8,128)}), f32[32,2,384,24]{2,3,1,0:T(8,128)S(1)}, u32[]{:S(2)}, u32[]{:S(2)}) %all-to-all-start) | async-done | bytes 2359328 | tf_op jit(solution)/shard_map/all_to_all | solution.py:17
  106.2 0.7 reduce_sum.9
  106.9 0.0 copy-start.1
  106.9 0.0 copy-start.2
  106.9 0.8 fusion.20
  107.8 9.6 %all_to_all.25 = bf16[8,384,24]{1,2,0:T(8,128)(2,1)S(1)} all-to-all(bf16[8,384,24]{1,2,0:T(8,128)(2,1)S(1)} %broadcast_in_dim.16), channel_id=1, replica_groups=mesh['row'=8,'z'=8,'x'=4] {'row'}, dimensions={0} | all-to-all | bytes 294912 | tf_op jit(solution)/shard_map/all_to_all | solution.py:29
  117.4 11.1 %all-gather.2.cloned.1.call-done = bf16[3,3072,384]{2,1,0:T(8,128)(2,1)} async-done(((bf16[3,96,384]{2,1,0:T(8,128)(2,1)}), bf16[3,3072,384]{2,1,0:T(8,128)(2,1)}) %all-gather.2.cloned.1.call-update) | async-done | bytes 7077904 | tf_op jit(solution)/shard_map/all_gather | solution.py:46
  128.4 2.1 %fusion.15 = bf16[384,24]{0,1:T(8,128)(2,1)S(1)} fusion(bf16[3072,24]{0,1:T(8,128)(2,1)S(1)} %bitcast.68, bf16[3,3072,384]{2,1,0:T(8,128)(2,1)} %all-gather.2.cloned.1.call-done), kind=kOutput, calls=%fused_computation.14 | convolution fusion | flops 56632320 | bytes 2525184 | tf_op jit(solution)/shard_map/dot_general | solution.py:37
  130.6 9.5 %all_to_all.26 = bf16[8,384,24]{1,2,0:T(8,128)(2,1)S(1)} all-to-all(bf16[8,384,24]{1,2,0:T(8,128)(2,1)S(1)} %broadcast_in_dim.17), channel_id=1, replica_groups=mesh['row'=8,'z'=8,'x'=4] {'row'}, dimensions={0} | all-to-all | bytes 294912 | tf_op jit(solution)/shard_map/all_to_all | solution.py:29
  140.1 0.0 copy-done.1
  140.1 0.0 copy-done.2
  140.1 2.1 %fusion.14 = bf16[384,24]{0,1:T(8,128)(2,1)S(1)} fusion(bf16[3072,24]{0,1:T(8,128)(2,1)S(1)} %bitcast.69, bf16[3,3072,384]{2,1,0:T(8,128)(2,1)} %all-gather.2.cloned.1.call-done, f32[2,384,24]{1,2,0:T(8,128)S(1)} %copy-done.2, f32[2,384,24]{1,2,0:T(8,128)S(1)} %copy-done.1), kind=kOutput, calls=%fused_computation.13 | convolution fusion | flops 56650752 | bytes 2598912 | tf_op jit(solution)/shard_map/dot_general | solution.py:37
  142.3 8.7 %all_to_all.27 = bf16[8,384,24]{1,2,0:T(8,128)(2,1)S(1)} all-to-all(bf16[8,384,24]{1,2,0:T(8,128)(2,1)S(1)} %broadcast_in_dim.18), channel_id=1, replica_groups=mesh['row'=8,'z'=8,'x'=4] {'row'}, dimensions={0} | all-to-all | bytes 294912 | tf_op jit(solution)/shard_map/all_to_all | solution.py:29
  150.9 2.1 %fusion.17 = bf16[1,384,24]{1,2,0:T(8,128)(2,1)S(1)} fusion(bf16[3072,24]{0,1:T(8,128)(2,1)S(1)} %bitcast.70, bf16[3,3072,384]{2,1,0:T(8,128)(2,1)} %all-gather.2.cloned.1.call-done), kind=kOutput, calls=%fused_computation.16 | convolution fusion | flops 56632320 | bytes 2525184 | tf_op jit(solution)/shard_map/dot_general | solution.py:37
  153.0 12.1 %all_gather.7 = bf16[2,384,96]{1,2,0:T(8,128)(2,1)S(1)} all-gather(bf16[2,384,24]{1,2,0:T(8,128)(2,1)S(1)} %pad_maximum_fusion.1), channel_id=1, replica_groups=mesh['row'=8,'z'=8,'x'=4] {'x'}, dimensions={2}, use_global_device_ids=true | all-gather | bytes 184320 | tf_op jit(solution)/shard_map/all_gather | solution.py:63
  165.1 0.1 broadcast_in_dim.19
  165.2 33.7 %all_to_all.28 = bf16[8,2,384,96]{2,3,1,0:T(8,128)(2,1)S(1)} all-to-all(bf16[8,2,384,96]{2,3,1,0:T(8,128)(2,1)S(1)} %broadcast_in_dim.19), channel_id=1, replica_groups=mesh['row'=8,'z'=8,'x'=4] {'z'}, dimensions={0} | all-to-all | bytes 2359296 | tf_op jit(solution)/shard_map/all_to_all | solution.py:29
  198.9 0.1 copy.38
  199.1 1.5 copy.39
  (7 shorter events, 0.1 us)
Async XLA Ops:
  6.5 29.7 %copy-start = (bf16[2,384,768]{2,1,0:T(8,128)(2,1)S(1)}, bf16[2,384,768]{2,1,0:T(8,128)(2,1)}, u32[]{:S(2)}) copy-start(bf16[2,384,768]{2,1,0:T(8,128)(2,1)} %param.7) | copy-start | bytes 3538948
  6.5 121.9 %all-gather.2.cloned.1.call-start = ((), (), s32[]{:S(2)}) async-start(), calls=%async_computation.5 | async-start | bytes 7299072 | tf_op jit(solution)/shard_map/all_gather | solution.py:46
  24.9 81.3 %all-to-all-start = ((f32[32,2,384,24]{2,3,1,0:T(8,128)}), f32[32,2,384,24]{2,3,1,0:T(8,128)S(1)}, u32[]{:S(2)}, u32[]{:S(2)}) async-start(f32[32,2,384,24]{2,3,1,0:T(8,128)} %copy.34), calls=%async_computation | async-start | bytes 4718592 | tf_op jit(solution)/shard_map/all_to_all | solution.py:17
  106.9 33.2 %copy-start.1 = (f32[2,384,24]{1,2,0:T(8,128)S(1)}, f32[2,384,24]{1,2,0:T(8,128)}, u32[]{:S(2)}) copy-start(f32[2,384,24]{1,2,0:T(8,128)} %convert_element_type.18) | copy-start | bytes 221188
  106.9 33.2 %copy-start.2 = (f32[2,384,24]{1,2,0:T(8,128)S(1)}, f32[2,384,24]{1,2,0:T(8,128)}, u32[]{:S(2)}) copy-start(f32[2,384,24]{1,2,0:T(8,128)} %reduce_sum.9) | copy-start | bytes 221188
Sparse Core Ops, SparseCore 0:
  9.9 118.4 all-gather.1

commit v8 on v5

--- a/solution.py
+++ b/solution.py
@@ -1,7 +1,9 @@
 import jax
 import jax.numpy as jnp
 from jax import lax
-from jax.sharding import PartitionSpec as P
+from jax.sharding import Mesh, PartitionSpec as P
+
+ROW = ("y", "core")
 
 
 def in_blocks(array, dim, length):
@@ -49,7 +51,8 @@
     rhs_share = lax.dynamic_slice_in_dim(rhs, share_start, share_width, 2).astype(jnp.float32)
 
     def apply_share(left_block, vector_rows):
-        full_vector = collect(vector_rows, "row", 0)
+        on_chip = lax.all_gather(vector_rows, "core", axis=0, tiled=True)
+        full_vector = collect(on_chip, "y", 0)
         return local_product(left_block, full_vector)
 
     first_reduced = (rhs_share[0] - shares[0]).astype(jnp.bfloat16)
@@ -62,16 +65,18 @@
 
 
 def solution(mesh):
+    nrow, ncol = mesh.devices.shape
+    fine = Mesh(mesh.devices.reshape(nrow // 2, 2, ncol), ("y", "core", "col"))
     return jax.shard_map(
         on_device,
-        mesh=mesh,
+        mesh=fine,
         in_specs=(
             P("col", None),
-            P("col", None, "row"),
-            P(None, "row", None),
-            P("col", "row"),
-            P(None, "col", "row"),
+            P("col", None, ROW),
+            P(None, ROW, None),
+            P("col", ROW),
+            P(None, "col", ROW),
         ),
-        out_specs=P(None, "row", None),
+        out_specs=P(None, ROW, None),
         check_vma=False,
     )

time: 202 us -> 204 us (level)
  blocking collectives: 67.1 us -> 71.4 us
    all_gather x0 -> x3, blocking collectives: none -> 5.49 us  [apply_share(): on_chip = lax.all_gather(vector_rows, 'core', axis=0, tiled=True)]
where the time goes in v8:
time: 204 us
  waiting for transfers between devices  75.6 us (37%)
  blocking collectives  71.4 us (35%)
  local copies, waits for them, and re-layouts  13.7 us (7%)
  between operations  13.5 us (7%)
  matrix products  13.3 us (7%)
  starting transfers between devices  11.3 us (6%)
  other arithmetic  4.75 us (2%)
    all_to_all x1, waiting for transfers between devices, sum_at_owner(): lax.all_to_all(in_blocks(array, dim, length), axis, 0, 0, tiled=True)  66.1 us
    all_to_all x4, blocking collectives, sent_to_all(): return lax.all_to_all(copies, axis, split_axis=0, concat_axis=0, tiled=True)  65.9 us
    dot_general x4, matrix products, local_product(): lax.dot_general(left_block, right_rows, (((0,), (0,)), ((), ())), preferr...  13.3 us
    all_to_all x1, starting transfers between devices, sum_at_owner(): lax.all_to_all(in_blocks(array, dim, length), axis, 0, 0, tiled=True)  11.3 us
    all_gather x1, waiting for transfers between devices, on_device(): whole_blocks = lax.all_gather(stacked, 'col', axis=1, tiled=True)  9.48 us
    unnamed x8, local copies, waits for them, and re-layouts  8.29 us
    all_gather x3, blocking collectives, apply_share(): on_chip = lax.all_gather(vector_rows, 'core', axis=0, tiled=True)  5.49 us
  transfers between devices with their start and end apart: 2, of which 2 were waited for; matrix products, arithmetic and copies ran while one was open for 11% of the time, Pallas kernels for 0%

profile of v8, /device:TPU:8, one launch (start us, length us, event | category | flops | bytes accessed | tf_op | source)
XLA Modules:
  0.0 203.6 jit_solution(1825309487204663510)
XLA Ops:
  6.5 0.0 copy-start
  6.5 0.0 all-gather.3.cloned.1.call-start
  6.5 1.8 pad_maximum_fusion
  8.3 0.0 all-gather.3.cloned.1.call-update
  8.3 6.6 %copy.31 = bf16[2880,768]{0,1:T(8,128)(2,1)} copy(bf16[2880,768]{1,0:T(8,128)(2,1)} %param.5) | data formatting | bytes 8847360 | tf_op args[0]
  14.9 7.1 %fusion.8 = f32[32,2,384,24]{2,0,3,1:T(8,128)S(1)} fusion(bf16[32,24,2880]{2,1,0:T(8,128)(2,1)} %bitcast.63, bf16[2880,2,384]{2,1,0:T(2,128)(2,1)} %param.6), kind=kOutput, calls=%fused_computation.11 | convolution fusion | flops 3397386240 | bytes 11206656 | tf_op jit(solution)/shard_map/dot_general | solution.py:37
  22.0 2.8 %copy.34 = f32[32,2,384,24]{2,3,1,0:T(8,128)} copy(f32[32,2,384,24]{2,0,3,1:T(8,128)S(1)} %fusion.8) | data formatting | bytes 4718592 | tf_op jit(solution)/shard_map/transpose | solution.py:12
  24.9 11.3 %all-to-all-start = ((f32[32,2,384,24]{2,3,1,0:T(8,128)}), f32[32,2,384,24]{2,3,1,0:T(8,128)S(1)}, u32[]{:S(2)}, u32[]{:S(2)}) async-start(f32[32,2,384,24]{2,3,1,0:T(8,128)} %copy.34), calls=%async_computation | async-start | bytes 4718592 | tf_op jit(solution)/shard_map/all_to_all | solution.py:17
  36.2 0.0 copy-done
  36.2 0.8 constant_dynamic-slice_fusion
  37.0 1.7 copy.43
  38.7 1.4 convert_element_type.18
  40.1 66.1 %all-to-all-done = f32[32,2,384,24]{2,3,1,0:T(8,128)S(1)} async-done(((f32[32,2,384,24]{2,3,1,0:T(8,128)}), f32[32,2,384,24]{2,3,1,0:T(8,128)S(1)}, u32[]{:S(2)}, u32[]{:S(2)}) %all-to-all-start) | async-done | bytes 2359328 | tf_op jit(solution)/shard_map/all_to_all | solution.py:17
  106.2 0.7 reduce_sum.9
  106.9 0.0 copy-start.1
  106.9 0.8 fusion.19
  107.8 1.8 all-gather
  109.6 9.4 %all_to_all.25 = bf16[4,768,24]{1,2,0:T(8,128)(2,1)S(1)} all-to-all(bf16[4,768,24]{1,2,0:T(8,128)(2,1)S(1)} %broadcast_in_dim.16), channel_id=1, replica_groups=mesh['y'=4,'core'=2,'col'=32] {'y'}, dimensions={0} | all-to-all | bytes 294912 | tf_op jit(solution)/shard_map/all_to_all | solution.py:29
  119.0 9.5 %all-gather.3.cloned.1.call-done = bf16[3,3072,384]{2,1,0:T(8,128)(2,1)} async-done(((bf16[3,96,384]{2,1,0:T(8,128)(2,1)}), bf16[3,3072,384]{2,1,0:T(8,128)(2,1)}) %all-gather.3.cloned.1.call-update) | async-done | bytes 7077904 | tf_op jit(solution)/shard_map/all_gather | solution.py:46
  128.4 2.1 %fusion.15 = bf16[384,24]{0,1:T(8,128)(2,1)S(1)} fusion(bf16[3072,24]{0,1:T(8,128)(2,1)S(1)} %bitcast.67, bf16[3,3072,384]{2,1,0:T(8,128)(2,1)} %all-gather.3.cloned.1.call-done), kind=kOutput, calls=%fused_computation.14 | convolution fusion | flops 56632320 | bytes 2525184 | tf_op jit(solution)/shard_map/dot_general | solution.py:37
  130.5 1.8 all_gather.14
  132.4 9.3 %all_to_all.26 = bf16[4,768,24]{1,2,0:T(8,128)(2,1)S(1)} all-to-all(bf16[4,768,24]{1,2,0:T(8,128)(2,1)S(1)} %broadcast_in_dim.17), channel_id=1, replica_groups=mesh['y'=4,'core'=2,'col'=32] {'y'}, dimensions={0} | all-to-all | bytes 294912 | tf_op jit(solution)/shard_map/all_to_all | solution.py:29
  141.7 0.0 copy-done.1
  141.7 0.0 copy-done.2
  141.7 2.1 %fusion.14 = bf16[384,24]{0,1:T(8,128)(2,1)S(1)} fusion(bf16[3072,24]{0,1:T(8,128)(2,1)S(1)} %bitcast.68, bf16[3,3072,384]{2,1,0:T(8,128)(2,1)} %all-gather.3.cloned.1.call-done, f32[2,384,24]{1,2,0:T(8,128)S(1)} %copy-done.2, f32[2,384,24]{1,2,0:T(8,128)S(1)} %copy-done.1), kind=kOutput, calls=%fused_computation.13 | convolution fusion | flops 56650752 | bytes 2598912 | tf_op jit(solution)/shard_map/dot_general | solution.py:37
  143.8 1.8 all_gather.15
  145.7 8.4 %all_to_all.27 = bf16[4,768,24]{1,2,0:T(8,128)(2,1)S(1)} all-to-all(bf16[4,768,24]{1,2,0:T(8,128)(2,1)S(1)} %broadcast_in_dim.18), channel_id=1, replica_groups=mesh['y'=4,'core'=2,'col'=32] {'y'}, dimensions={0} | all-to-all | bytes 294912 | tf_op jit(solution)/shard_map/all_to_all | solution.py:29
  154.1 2.1 %fusion.17 = bf16[1,384,24]{1,2,0:T(8,128)(2,1)S(1)} fusion(bf16[3072,24]{0,1:T(8,128)(2,1)S(1)} %bitcast.69, bf16[3,3072,384]{2,1,0:T(8,128)(2,1)} %all-gather.3.cloned.1.call-done), kind=kOutput, calls=%fused_computation.16 | convolution fusion | flops 56632320 | bytes 2525184 | tf_op jit(solution)/shard_map/dot_general | solution.py:37
  156.2 0.1 broadcast_in_dim.19
  156.3 38.8 %all_to_all.28 = bf16[32,2,384,24]{2,3,1,0:T(8,128)(2,1)S(1)} all-to-all(bf16[32,2,384,24]{2,3,1,0:T(8,128)(2,1)S(1)} %broadcast_in_dim.19), channel_id=1, replica_groups=mesh['y'=4,'core'=2,'col'=32] {'col'}, dimensions={0} | all-to-all | bytes 2359296 | tf_op jit(solution)/shard_map/all_to_all | solution.py:29
  195.1 0.1 copy.38
  195.3 1.5 copy.39
  (8 shorter events, 0.1 us)
Async XLA Ops:
  6.5 29.7 %copy-start = (bf16[2,384,768]{2,1,0:T(8,128)(2,1)S(1)}, bf16[2,384,768]{2,1,0:T(8,128)(2,1)}, u32[]{:S(2)}) copy-start(bf16[2,384,768]{2,1,0:T(8,128)(2,1)} %param.7) | copy-start | bytes 3538948
  6.5 121.9 %all-gather.3.cloned.1.call-start = ((), (), s32[]{:S(2)}) async-start(), calls=%async_computation.5 | async-start | bytes 7299072 | tf_op jit(solution)/shard_map/all_gather | solution.py:46
  24.9 81.3 %all-to-all-start = ((f32[32,2,384,24]{2,3,1,0:T(8,128)}), f32[32,2,384,24]{2,3,1,0:T(8,128)S(1)}, u32[]{:S(2)}, u32[]{:S(2)}) async-start(f32[32,2,384,24]{2,3,1,0:T(8,128)} %copy.34), calls=%async_computation | async-start | bytes 4718592 | tf_op jit(solution)/shard_map/all_to_all | solution.py:17
  106.9 34.8 %copy-start.1 = (f32[2,384,24]{1,2,0:T(8,128)S(1)}, f32[2,384,24]{1,2,0:T(8,128)}, u32[]{:S(2)}) copy-start(f32[2,384,24]{1,2,0:T(8,128)} %convert_element_type.18) | copy-start | bytes 221188
  106.9 34.8 %copy-start.2 = (f32[2,384,24]{1,2,0:T(8,128)S(1)}, f32[2,384,24]{1,2,0:T(8,128)}, u32[]{:S(2)}) copy-start(f32[2,384,24]{1,2,0:T(8,128)} %reduce_sum.9) | copy-start | bytes 221188
Sparse Core Ops, SparseCore 0:
  9.9 118.4 all-gather.2

commit v9 on v5

--- a/solution.py
+++ b/solution.py
@@ -45,7 +45,9 @@
     depth, blocks, rows = lower_prior.shape
     both_terms = local_product(lower_prior.reshape(depth, blocks * rows), prior_solved)
     both_terms = both_terms.reshape(blocks, rows, rhs.shape[2])
-    shares = sum_at_owner(both_terms, "col", 2)
+    length = lax.axis_size("col")
+    blocks_out = lax.all_to_all(in_blocks(both_terms.astype(jnp.bfloat16), 2, length), "col", 0, 0, tiled=True)
+    shares = jnp.sum(blocks_out.astype(jnp.float32), axis=0)
     rhs_share = lax.dynamic_slice_in_dim(rhs, share_start, share_width, 2).astype(jnp.float32)
 
     def apply_share(left_block, vector_rows):

time: 202 us -> 181 us (0.90)
  waiting for transfers between devices: 77.2 us -> 57.3 us
  other arithmetic: 4.75 us -> 1.95 us
  local copies, waits for them, and re-layouts: 13.7 us -> 16.3 us
    all_to_all x1, waiting for transfers between devices: 66.1 us -> 35.2 us  [on_device(): lax.all_to_all(in_blocks(both_terms.astype(jnp.bfloat16), 2, length), 'co...]
    dot_general x0 -> x1, local copies, waits for them, and re-layouts: none -> 12.4 us  [local_product(): lax.dot_general(left_block, right_rows, (((0,), (0,)), ((), ())), preferr...]
    all_gather x1, waiting for transfers between devices: 11.1 us -> 22.1 us  [on_device(): whole_blocks = lax.all_gather(stacked, 'col', axis=1, tiled=True)]
    unnamed x8 -> x3, local copies, waits for them, and re-layouts: 8.29 us -> 0.12 us
  transfers between devices with their start and end apart: 2 -> 2, of which waited for: 2 -> 2; matrix products, arithmetic and copies ran while one was open for 11% -> 12% of each run, Pallas kernels for 0% -> 0%
where the time goes in v9:
time: 181 us; the launch traced here: 180 us
  blocking collectives  65.6 us (36%)
  waiting for transfers between devices  57.3 us (32%)
  local copies, waits for them, and re-layouts  16.3 us (9%)
  matrix products  13.7 us (8%)
  between operations  13.5 us (7%)
  starting transfers between devices  11.4 us (6%)
  other arithmetic  1.95 us (1%)
    all_to_all x4, blocking collectives, sent_to_all(): return lax.all_to_all(copies, axis, split_axis=0, concat_axis=0, tiled=True)  65.6 us
    all_to_all x1, waiting for transfers between devices, on_device(): lax.all_to_all(in_blocks(both_terms.astype(jnp.bfloat16), 2, length), 'co...  35.2 us
    all_gather x1, waiting for transfers between devices, on_device(): whole_blocks = lax.all_gather(stacked, 'col', axis=1, tiled=True)  22.1 us
    dot_general x4, matrix products, local_product(): lax.dot_general(left_block, right_rows, (((0,), (0,)), ((), ())), preferr...  13.7 us
    dot_general x1, local copies, waits for them, and re-layouts, local_product(): lax.dot_general(left_block, right_rows, (((0,), (0,)), ((), ())), preferr...  12.4 us
    all_to_all x1, starting transfers between devices, on_device(): lax.all_to_all(in_blocks(both_terms.astype(jnp.bfloat16), 2, length), 'co...  11.4 us
  transfers between devices with their start and end apart: 2, of which 2 were waited for; matrix products, arithmetic and copies ran while one was open for 12% of the time, Pallas kernels for 0%

profile of v9, /device:TPU:8, one launch (start us, length us, event | category | flops | bytes accessed | tf_op | source)
XLA Modules:
  0.0 179.9 jit_solution(4644803607920628770)
XLA Ops:
  6.5 0.0 copy-start
  6.5 0.0 all-gather.2.cloned.1.call-start
  6.5 1.8 pad_maximum_fusion
  8.3 0.0 all-gather.2.cloned.1.call-update
  8.3 12.4 %copy.39 = bf16[2880,2,384]{0,2,1:T(8,128)(2,1)} copy(bf16[2880,2,384]{2,1,0:T(2,128)(2,1)} %param.6) | data formatting | bytes 8847360 | tf_op jit(solution)/shard_map/dot_general | solution.py:35
  20.8 7.4 %fusion.6 = bf16[2,384,768]{2,1,0:T(8,128)(2,1)S(1)} fusion(bf16[2880,768]{1,0:T(8,128)(2,1)} %param.5, bf16[2880,2,384]{0,2,1:T(8,128)(2,1)} %copy.39), kind=kOutput, calls=%fused_computation.10 | convolution fusion | flops 3397976064 | bytes 10027008 | tf_op jit(solution)/shard_map/dot_general | solution.py:35
  28.2 0.7 copy.29
  28.9 1.1 copy.30
  30.1 11.4 %all-to-all-start = ((bf16[32,2,384,24]{2,3,1,0:T(8,128)(2,1)}), bf16[32,2,384,24]{2,3,1,0:T(8,128)(2,1)S(1)}, u32[]{:S(2)}, u32[]{:S(2)}) async-start(bf16[32,2,384,24]{2,3,1,0:T(8,128)(2,1)} %copy.30), calls=%async_computation | async-start | bytes 2359296 | tf_op jit(solution)/shard_map/all_to_all | solution.py:49
  41.5 0.0 copy-done
  41.5 0.1 constant_dynamic-slice_fusion
  41.7 0.1 copy.40
  41.8 35.2 %all-to-all-done = bf16[32,2,384,24]{2,3,1,0:T(8,128)(2,1)S(1)} async-done(((bf16[32,2,384,24]{2,3,1,0:T(8,128)(2,1)}), bf16[32,2,384,24]{2,3,1,0:T(8,128)(2,1)S(1)}, u32[]{:S(2)}, u32[]{:S(2)}) %all-to-all-start) | async-done | bytes 1179680 | tf_op jit(solution)/shard_map/all_to_all | solution.py:49
  77.0 0.2 convert_reduce_fusion
  77.2 9.3 %all_to_all.25 = bf16[8,384,24]{1,2,0:T(8,128)(2,1)S(1)} all-to-all(bf16[8,384,24]{1,2,0:T(8,128)(2,1)S(1)} %broadcast_in_dim.16), channel_id=1, replica_groups=mesh['row'=8,'col'=32] {'row'}, dimensions={0} | all-to-all | bytes 294912 | tf_op jit(solution)/shard_map/all_to_all | solution.py:27
  86.6 22.1 %all-gather.2.cloned.1.call-done = bf16[3,3072,384]{2,1,0:T(8,128)(2,1)} async-done(((bf16[3,96,384]{2,1,0:T(8,128)(2,1)}), bf16[3,3072,384]{2,1,0:T(8,128)(2,1)}) %all-gather.2.cloned.1.call-update) | async-done | bytes 7077904 | tf_op jit(solution)/shard_map/all_gather | solution.py:44
  108.7 2.1 %fusion.13 = bf16[384,24]{0,1:T(8,128)(2,1)S(1)} fusion(bf16[3072,24]{0,1:T(8,128)(2,1)S(1)} %bitcast.63, bf16[3,3072,384]{2,1,0:T(8,128)(2,1)} %all-gather.2.cloned.1.call-done), kind=kOutput, calls=%fused_computation.13 | convolution fusion | flops 56632320 | bytes 2525184 | tf_op jit(solution)/shard_map/dot_general | solution.py:35
  110.8 9.4 %all_to_all.26 = bf16[8,384,24]{1,2,0:T(8,128)(2,1)S(1)} all-to-all(bf16[8,384,24]{1,2,0:T(8,128)(2,1)S(1)} %broadcast_in_dim.17), channel_id=1, replica_groups=mesh['row'=8,'col'=32] {'row'}, dimensions={0} | all-to-all | bytes 294912 | tf_op jit(solution)/shard_map/all_to_all | solution.py:27
  120.2 2.1 %fusion.12 = bf16[384,24]{0,1:T(8,128)(2,1)S(1)} fusion(bf16[3072,24]{0,1:T(8,128)(2,1)S(1)} %bitcast.64, bf16[3,3072,384]{2,1,0:T(8,128)(2,1)} %all-gather.2.cloned.1.call-done, f32[2,384,24]{1,2,0:T(8,128)S(1)} %convert_reduce_fusion, f32[2,384,24]{1,2,0:T(8,128)S(1)} %convert_element_type.24), kind=kOutput, calls=%fused_computation.12 | convolution fusion | flops 56650752 | bytes 2598912 | tf_op jit(solution)/shard_map/dot_general | solution.py:35
  122.3 8.7 %all_to_all.27 = bf16[8,384,24]{1,2,0:T(8,128)(2,1)S(1)} all-to-all(bf16[8,384,24]{1,2,0:T(8,128)(2,1)S(1)} %broadcast_in_dim.18), channel_id=1, replica_groups=mesh['row'=8,'col'=32] {'row'}, dimensions={0} | all-to-all | bytes 294912 | tf_op jit(solution)/shard_map/all_to_all | solution.py:27
  131.0 2.1 %fusion.15 = bf16[1,384,24]{1,2,0:T(8,128)(2,1)S(1)} fusion(bf16[3072,24]{0,1:T(8,128)(2,1)S(1)} %bitcast.65, bf16[3,3072,384]{2,1,0:T(8,128)(2,1)} %all-gather.2.cloned.1.call-done), kind=kOutput, calls=%fused_computation.15 | convolution fusion | flops 56632320 | bytes 2525184 | tf_op jit(solution)/shard_map/dot_general | solution.py:35
  133.1 0.1 broadcast_in_dim.19
  133.2 38.3 %all_to_all.28 = bf16[32,2,384,24]{2,3,1,0:T(8,128)(2,1)S(1)} all-to-all(bf16[32,2,384,24]{2,3,1,0:T(8,128)(2,1)S(1)} %broadcast_in_dim.19), channel_id=1, replica_groups=mesh['row'=8,'col'=32] {'col'}, dimensions={0} | all-to-all | bytes 2359296 | tf_op jit(solution)/shard_map/all_to_all | solution.py:27
  171.5 0.1 copy.34
  171.6 1.5 copy.35
  (9 shorter events, 0.1 us)
Async XLA Ops:
  6.5 35.0 %copy-start = (bf16[2,384,768]{2,1,0:T(8,128)(2,1)S(1)}, bf16[2,384,768]{2,1,0:T(8,128)(2,1)}, u32[]{:S(2)}) copy-start(bf16[2,384,768]{2,1,0:T(8,128)(2,1)} %param.7) | copy-start | bytes 3538948
  6.5 102.1 %all-gather.2.cloned.1.call-start = ((), (), s32[]{:S(2)}) async-start(), calls=%async_computation.5 | async-start | bytes 7299072 | tf_op jit(solution)/shard_map/all_gather | solution.py:44
  30.1 47.0 %all-to-all-start = ((bf16[32,2,384,24]{2,3,1,0:T(8,128)(2,1)}), bf16[32,2,384,24]{2,3,1,0:T(8,128)(2,1)S(1)}, u32[]{:S(2)}, u32[]{:S(2)}) async-start(bf16[32,2,384,24]{2,3,1,0:T(8,128)(2,1)} %copy.30), calls=%async_computation | async-start | bytes 2359296 | tf_op jit(solution)/shard_map/all_to_all | solution.py:49
Sparse Core Ops, SparseCore 0:
  9.9 98.6 all-gather.1

commit v10 on v5

--- a/solution.py
+++ b/solution.py
@@ -40,9 +40,11 @@
 def on_device(prior_solved, lower_prior, rhs, coupling, inverse_diag):
     share_width = rhs.shape[2] // lax.axis_size("col")
     share_start = lax.axis_index("col") * share_width
-    stacked = jnp.concatenate([inverse_diag, coupling[None]], axis=0)
-    whole_blocks = lax.all_gather(stacked, "col", axis=1, tiled=True)
-    depth, blocks, rows = lower_prior.shape
+    rows = coupling.shape[1]
+    side = jnp.concatenate([inverse_diag[0], inverse_diag[1], coupling], axis=1)
+    whole = lax.all_gather(side, "col", axis=0, tiled=True)
+    whole_blocks = [whole[:, k * rows : (k + 1) * rows] for k in range(3)]
+    depth, blocks, _ = lower_prior.shape
     both_terms = local_product(lower_prior.reshape(depth, blocks * rows), prior_solved)
     both_terms = both_terms.reshape(blocks, rows, rhs.shape[2])
     shares = sum_at_owner(both_terms, "col", 2)

time: 202 us -> 202 us (level)
  no operation moved by 1% of the time
where the time goes in v10:
time: 202 us
  waiting for transfers between devices  76.7 us (38%)
  blocking collectives  67.4 us (33%)
  local copies, waits for them, and re-layouts  14.7 us (7%)
  between operations  13.5 us (7%)
  matrix products  13.3 us (7%)
  starting transfers between devices  11.3 us (6%)
  other arithmetic  4.6 us (2%)
    all_to_all x4, blocking collectives, sent_to_all(): return lax.all_to_all(copies, axis, split_axis=0, concat_axis=0, tiled=True)  67.4 us
    all_to_all x1, waiting for transfers between devices, sum_at_owner(): lax.all_to_all(in_blocks(array, dim, length), axis, 0, 0, tiled=True)  66.9 us
    dot_general x4, matrix products, local_product(): lax.dot_general(left_block, right_rows, (((0,), (0,)), ((), ())), preferr...  13.3 us
    all_to_all x1, starting transfers between devices, sum_at_owner(): lax.all_to_all(in_blocks(array, dim, length), axis, 0, 0, tiled=True)  11.3 us
    all_gather x1, waiting for transfers between devices, on_device(): whole = lax.all_gather(side, 'col', axis=0, tiled=True)  9.81 us
    unnamed x8, local copies, waits for them, and re-layouts  8.27 us
  transfers between devices with their start and end apart: 2, of which 2 were waited for; matrix products, arithmetic and copies ran while one was open for 11% of the time, Pallas kernels for 0%

profile of v10, /device:TPU:8, one launch (start us, length us, event | category | flops | bytes accessed | tf_op | source)
XLA Modules:
  0.0 201.7 jit_solution(13906891392278558842)
XLA Ops:
  6.5 0.0 copy-start
  6.5 0.0 all-gather.2.cloned.1.call-start
  6.5 1.0 slice_bitcast_fusion.1
  7.6 1.6 pad_maximum_fusion
  9.2 0.0 all-gather.2.cloned.1.call-update
  9.2 6.6 %copy.31 = bf16[2880,768]{0,1:T(8,128)(2,1)} copy(bf16[2880,768]{1,0:T(8,128)(2,1)} %param.5) | data formatting | bytes 8847360 | tf_op args[0]
  15.8 7.1 %fusion.11 = f32[32,2,384,24]{2,0,3,1:T(8,128)S(1)} fusion(bf16[32,24,2880]{2,1,0:T(8,128)(2,1)} %bitcast.48, bf16[2880,2,384]{2,1,0:T(2,128)(2,1)} %param.6), kind=kOutput, calls=%fused_computation.11 | convolution fusion | flops 3397386240 | bytes 11206656 | tf_op jit(solution)/shard_map/dot_general | solution.py:35
  22.9 2.8 %copy.34 = f32[32,2,384,24]{2,3,1,0:T(8,128)} copy(f32[32,2,384,24]{2,0,3,1:T(8,128)S(1)} %fusion.11) | data formatting | bytes 4718592 | tf_op jit(solution)/shard_map/transpose | solution.py:10
  25.7 11.3 %all-to-all-start = ((f32[32,2,384,24]{2,3,1,0:T(8,128)}), f32[32,2,384,24]{2,3,1,0:T(8,128)S(1)}, u32[]{:S(2)}, u32[]{:S(2)}) async-start(f32[32,2,384,24]{2,3,1,0:T(8,128)} %copy.34), calls=%async_computation | async-start | bytes 4718592 | tf_op jit(solution)/shard_map/all_to_all | solution.py:15
  37.1 0.0 copy-done
  37.1 0.8 constant_dynamic-slice_fusion
  37.9 1.6 copy.43
  39.5 1.4 convert_element_type.18
  40.9 66.9 %all-to-all-done = f32[32,2,384,24]{2,3,1,0:T(8,128)S(1)} async-done(((f32[32,2,384,24]{2,3,1,0:T(8,128)}), f32[32,2,384,24]{2,3,1,0:T(8,128)S(1)}, u32[]{:S(2)}, u32[]{:S(2)}) %all-to-all-start) | async-done | bytes 2359328 | tf_op jit(solution)/shard_map/all_to_all | solution.py:15
  107.8 0.8 reduce_sum.9
  108.6 0.0 copy-start.1
  108.6 0.0 copy-start.2
  108.6 0.8 fusion.33
  109.5 9.7 %all_to_all.25 = bf16[8,384,24]{1,2,0:T(8,128)(2,1)S(1)} all-to-all(bf16[8,384,24]{1,2,0:T(8,128)(2,1)S(1)} %broadcast_in_dim.12), channel_id=1, replica_groups=mesh['row'=8,'col'=32] {'row'}, dimensions={0} | all-to-all | bytes 294912 | tf_op jit(solution)/shard_map/all_to_all | solution.py:27
  119.2 9.8 %all-gather.2.cloned.1.call-done = bf16[3072,1152]{1,0:T(8,128)(2,1)} async-done(((bf16[96,1152]{1,0:T(8,128)(2,1)}), bf16[3072,1152]{1,0:T(8,128)(2,1)}) %all-gather.2.cloned.1.call-update) | async-done | bytes 7077904 | tf_op jit(solution)/shard_map/all_gather | solution.py:45
  129.0 2.1 %fusion.22 = bf16[384,24]{0,1:T(8,128)(2,1)S(1)} fusion(bf16[3072,24]{0,1:T(8,128)(2,1)S(1)} %bitcast.52, bf16[3072,1152]{1,0:T(8,128)(2,1)} %all-gather.2.cloned.1.call-done), kind=kOutput, calls=%fused_computation.14 | convolution fusion | flops 56632320 | bytes 2525184 | tf_op jit(solution)/shard_map/dot_general | solution.py:35
  131.1 9.5 %all_to_all.26 = bf16[8,384,24]{1,2,0:T(8,128)(2,1)S(1)} all-to-all(bf16[8,384,24]{1,2,0:T(8,128)(2,1)S(1)} %broadcast_in_dim.13), channel_id=1, replica_groups=mesh['row'=8,'col'=32] {'row'}, dimensions={0} | all-to-all | bytes 294912 | tf_op jit(solution)/shard_map/all_to_all | solution.py:27
  140.7 0.0 copy-done.1
  140.7 0.0 copy-done.2
  140.7 2.1 %fusion.19 = bf16[384,24]{0,1:T(8,128)(2,1)S(1)} fusion(bf16[3072,24]{0,1:T(8,128)(2,1)S(1)} %bitcast.53, bf16[3072,1152]{1,0:T(8,128)(2,1)} %all-gather.2.cloned.1.call-done, f32[2,384,24]{1,2,0:T(8,128)S(1)} %copy-done.2, f32[2,384,24]{1,2,0:T(8,128)S(1)} %copy-done.1), kind=kOutput, calls=%fused_computation.13 | convolution fusion | flops 56650752 | bytes 2598912 | tf_op jit(solution)/shard_map/dot_general | solution.py:35
  142.8 8.7 %all_to_all.27 = bf16[8,384,24]{1,2,0:T(8,128)(2,1)S(1)} all-to-all(bf16[8,384,24]{1,2,0:T(8,128)(2,1)S(1)} %broadcast_in_dim.14), channel_id=1, replica_groups=mesh['row'=8,'col'=32] {'row'}, dimensions={0} | all-to-all | bytes 294912 | tf_op jit(solution)/shard_map/all_to_all | solution.py:27
  151.5 2.1 %fusion.28 = bf16[1,384,24]{1,2,0:T(8,128)(2,1)S(1)} fusion(bf16[3072,24]{0,1:T(8,128)(2,1)S(1)} %bitcast.54, bf16[3072,1152]{1,0:T(8,128)(2,1)} %all-gather.2.cloned.1.call-done), kind=kOutput, calls=%fused_computation.16 | convolution fusion | flops 56632320 | bytes 2525184 | tf_op jit(solution)/shard_map/dot_general | solution.py:35
  153.6 0.1 broadcast_in_dim.15
  153.7 39.5 %all_to_all.28 = bf16[32,2,384,24]{2,3,1,0:T(8,128)(2,1)S(1)} all-to-all(bf16[32,2,384,24]{2,3,1,0:T(8,128)(2,1)S(1)} %broadcast_in_dim.15), channel_id=1, replica_groups=mesh['row'=8,'col'=32] {'col'}, dimensions={0} | all-to-all | bytes 2359296 | tf_op jit(solution)/shard_map/all_to_all | solution.py:27
  193.2 0.1 copy.38
  193.4 1.5 copy.39
  (7 shorter events, 0.1 us)
Async XLA Ops:
  6.5 30.5 %copy-start = (bf16[2,384,768]{2,1,0:T(8,128)(2,1)S(1)}, bf16[2,384,768]{2,1,0:T(8,128)(2,1)}, u32[]{:S(2)}) copy-start(bf16[2,384,768]{2,1,0:T(8,128)(2,1)} %param.7) | copy-start | bytes 3538948
  6.5 122.5 %all-gather.2.cloned.1.call-start = ((), (), s32[]{:S(2)}) async-start(), calls=%async_computation.5 | async-start | bytes 7299072 | tf_op jit(solution)/shard_map/all_gather | solution.py:45
  25.7 82.1 %all-to-all-start = ((f32[32,2,384,24]{2,3,1,0:T(8,128)}), f32[32,2,384,24]{2,3,1,0:T(8,128)S(1)}, u32[]{:S(2)}, u32[]{:S(2)}) async-start(f32[32,2,384,24]{2,3,1,0:T(8,128)} %copy.34), calls=%async_computation | async-start | bytes 4718592 | tf_op jit(solution)/shard_map/all_to_all | solution.py:15
  108.6 32.1 %copy-start.1 = (f32[2,384,24]{1,2,0:T(8,128)S(1)}, f32[2,384,24]{1,2,0:T(8,128)}, u32[]{:S(2)}) copy-start(f32[2,384,24]{1,2,0:T(8,128)} %convert_element_type.18) | copy-start | bytes 221188
  108.6 32.1 %copy-start.2 = (f32[2,384,24]{1,2,0:T(8,128)S(1)}, f32[2,384,24]{1,2,0:T(8,128)}, u32[]{:S(2)}) copy-start(f32[2,384,24]{1,2,0:T(8,128)} %reduce_sum.9) | copy-start | bytes 221188
Sparse Core Ops, SparseCore 0:
  9.9 119.0 all-gather.1

commit v11 on v7

--- a/solution.py
+++ b/solution.py
@@ -47,7 +47,12 @@
     depth, blocks, rows = lower_prior.shape
     both_terms = local_product(lower_prior.reshape(depth, blocks * rows), prior_solved)
     both_terms = both_terms.reshape(blocks, rows, rhs.shape[2])
-    shares = sum_at_owner(both_terms, COL, 2)
+    nz, nx = lax.axis_size("z"), lax.axis_size("x")
+    per_x = both_terms.reshape(blocks, rows, nz, nx, share_width)
+    per_x = jnp.moveaxis(per_x, 3, 0)
+    along_x = jnp.sum(lax.all_to_all(per_x, "x", 0, 0, tiled=True), axis=0)
+    per_z = jnp.moveaxis(along_x.reshape(blocks, rows, nz, share_width), 2, 0)
+    shares = jnp.sum(lax.all_to_all(per_z, "z", 0, 0, tiled=True), axis=0)
     rhs_share = lax.dynamic_slice_in_dim(rhs, share_start, share_width, 2).astype(jnp.float32)
 
     def apply_share(left_block, vector_rows):
@@ -60,8 +65,7 @@
     second_reduced = (rhs_share[1] - shares[1] - cross_term).astype(jnp.bfloat16)
     second_solved = apply_share(whole_blocks[1], second_reduced).astype(jnp.bfloat16)
     solved_share = jnp.stack([first_solved, second_solved])
-    across_x = lax.all_gather(solved_share, "x", axis=2, tiled=True)
-    return collect(across_x, "z", 2)
+    return collect(solved_share, COL, 2)
 
 
 def solution(mesh):

time: 208 us -> 186 us (0.89)
  waiting for transfers between devices: 77.2 us -> 34.3 us
  blocking collectives: 73.5 us -> 104 us
  starting transfers between devices: 11.3 us -> 7.73 us
  local copies, waits for them, and re-layouts: 13.7 us -> 10.7 us
    all_to_all x1, waiting for transfers between devices: 66.1 us -> 24.9 us  [on_device(): shares = jnp.sum(lax.all_to_all(per_z, 'z', 0, 0, tiled=True), axis=0)]
    all_to_all x0 -> x1, blocking collectives: none -> 36.3 us  [on_device(): along_x = jnp.sum(lax.all_to_all(per_x, 'x', 0, 0, tiled=True), axis=0)]
    all_gather x1 -> x0, blocking collectives: 12.1 us -> none  [on_device(): across_x = lax.all_gather(solved_share, 'x', axis=2, tiled=True)]
    all_to_all x4, blocking collectives: 61.5 us -> 67.3 us  [sent_to_all(): return lax.all_to_all(copies, axis, split_axis=0, concat_axis=0, tiled=True)]
    all_to_all x1, starting transfers between devices: 11.3 us -> 7.73 us  [on_device(): shares = jnp.sum(lax.all_to_all(per_z, 'z', 0, 0, tiled=True), axis=0)]
    unnamed x8 -> x4, local copies, waits for them, and re-layouts: 8.29 us -> 6.7 us
  transfers between devices with their start and end apart: 2 -> 2, of which waited for: 2 -> 2; matrix products, arithmetic and copies ran while one was open for 11% -> 9% of each run, Pallas kernels for 0% -> 0%
where the time goes in v11:
time: 186 us
  blocking collectives  104 us (56%)
  waiting for transfers between devices  34.3 us (18%)
  between operations  13.5 us (7%)
  matrix products  13.3 us (7%)
  local copies, waits for them, and re-layouts  10.7 us (6%)
  starting transfers between devices  7.73 us (4%)
  other arithmetic  2.8 us (2%)
    all_to_all x4, blocking collectives, sent_to_all(): return lax.all_to_all(copies, axis, split_axis=0, concat_axis=0, tiled=True)  67.3 us
    all_to_all x1, blocking collectives, on_device(): along_x = jnp.sum(lax.all_to_all(per_x, 'x', 0, 0, tiled=True), axis=0)  36.3 us
    all_to_all x1, waiting for transfers between devices, on_device(): shares = jnp.sum(lax.all_to_all(per_z, 'z', 0, 0, tiled=True), axis=0)  24.9 us
    dot_general x4, matrix products, local_product(): lax.dot_general(left_block, right_rows, (((0,), (0,)), ((), ())), preferr...  13.3 us
    all_gather x1, waiting for transfers between devices, on_device(): whole_blocks = lax.all_gather(stacked, COL, axis=1, tiled=True)  9.42 us
    all_to_all x1, starting transfers between devices, on_device(): shares = jnp.sum(lax.all_to_all(per_z, 'z', 0, 0, tiled=True), axis=0)  7.73 us
    unnamed x4, local copies, waits for them, and re-layouts  6.7 us
  transfers between devices with their start and end apart: 2, of which 2 were waited for; matrix products, arithmetic and copies ran while one was open for 9% of the time, Pallas kernels for 0%

profile of v11, /device:TPU:8, one launch (start us, length us, event | category | flops | bytes accessed | tf_op | source)
XLA Modules:
  0.0 185.8 jit_solution(218872014612678964)
XLA Ops:
  6.5 0.0 copy-start
  6.5 0.0 all-gather.2.cloned.1.call-start
  6.5 1.8 pad_maximum_fusion
  8.3 0.0 all-gather.2.cloned.1.call-update
  8.3 6.6 %copy.31 = bf16[2880,768]{0,1:T(8,128)(2,1)} copy(bf16[2880,768]{1,0:T(8,128)(2,1)} %param.5) | data formatting | bytes 8847360 | tf_op args[0]
  14.9 7.0 %fusion.6 = f32[4,2,384,8,24]{2,4,0,3,1:T(8,128)S(1)} fusion(bf16[8,4,24,2880,1]{3,2,1,0,4:T(8,128)(2,1)} %bitcast.63, bf16[2880,2,384]{2,1,0:T(2,128)(2,1)} %param.6), kind=kOutput, calls=%fused_computation.9 | convolution fusion | flops 3397386240 | bytes 11206656 | tf_op jit(solution)/shard_map/dot_general | solution.py:37
  21.9 0.2 copy.33
  22.1 36.3 %all_to_all.30 = f32[4,2,384,8,24]{2,4,3,1,0:T(8,128)S(1)} all-to-all(f32[4,2,384,8,24]{2,4,3,1,0:T(8,128)S(1)} %copy.33), channel_id=1, replica_groups=mesh['row'=8,'z'=8,'x'=4] {'x'}, dimensions={0} | all-to-all | bytes 4718592 | tf_op jit(solution)/shard_map/all_to_all | solution.py:53
  58.3 1.0 reduce_sum.18
  59.3 1.9 %copy.35 = f32[8,2,384,24]{2,3,1,0:T(8,128)} copy(f32[8,2,384,24]{2,3,0,1:T(8,128)} %bitcast.64) | data formatting | bytes 1179648 | tf_op jit(solution)/shard_map/transpose | solution.py:54
  61.3 7.7 %all-to-all-start.1 = ((f32[8,2,384,24]{2,3,1,0:T(8,128)}), f32[8,2,384,24]{2,3,1,0:T(8,128)S(1)}, u32[]{:S(2)}, u32[]{:S(2)}) async-start(f32[8,2,384,24]{2,3,1,0:T(8,128)} %copy.35), calls=%async_computation.1 | async-start | bytes 1179648 | tf_op jit(solution)/shard_map/all_to_all | solution.py:55
  69.0 0.0 copy-done
  69.0 0.1 constant_dynamic-slice_fusion
  69.1 0.1 copy.45
  69.3 24.9 %all-to-all-done.1 = f32[8,2,384,24]{2,3,1,0:T(8,128)S(1)} async-done(((f32[8,2,384,24]{2,3,1,0:T(8,128)}), f32[8,2,384,24]{2,3,1,0:T(8,128)S(1)}, u32[]{:S(2)}, u32[]{:S(2)}) %all-to-all-start.1) | async-done | bytes 589856 | tf_op jit(solution)/shard_map/all_to_all | solution.py:55
  94.2 9.5 %all_to_all.31 = bf16[8,384,24]{1,2,0:T(8,128)(2,1)S(1)} all-to-all(bf16[8,384,24]{1,2,0:T(8,128)(2,1)S(1)} %broadcast_in_dim.16), channel_id=1, replica_groups=mesh['row'=8,'z'=8,'x'=4] {'row'}, dimensions={0} | all-to-all | bytes 294912 | tf_op jit(solution)/shard_map/all_to_all | solution.py:29
  103.7 9.4 %all-gather.2.cloned.1.call-done = bf16[3,3072,384]{2,1,0:T(8,128)(2,1)} async-done(((bf16[3,96,384]{2,1,0:T(8,128)(2,1)}), bf16[3,3072,384]{2,1,0:T(8,128)(2,1)}) %all-gather.2.cloned.1.call-update) | async-done | bytes 7077904 | tf_op jit(solution)/shard_map/all_gather | solution.py:46
  113.1 2.1 %fusion.11 = bf16[384,24]{0,1:T(8,128)(2,1)S(1)} fusion(bf16[3072,24]{0,1:T(8,128)(2,1)S(1)} %bitcast.68, bf16[3,3072,384]{2,1,0:T(8,128)(2,1)} %all-gather.2.cloned.1.call-done), kind=kOutput, calls=%fused_computation.12 | convolution fusion | flops 56632320 | bytes 2525184 | tf_op jit(solution)/shard_map/dot_general | solution.py:37
  115.2 9.4 %all_to_all.32 = bf16[8,384,24]{1,2,0:T(8,128)(2,1)S(1)} all-to-all(bf16[8,384,24]{1,2,0:T(8,128)(2,1)S(1)} %broadcast_in_dim.17), channel_id=1, replica_groups=mesh['row'=8,'z'=8,'x'=4] {'row'}, dimensions={0} | all-to-all | bytes 294912 | tf_op jit(solution)/shard_map/all_to_all | solution.py:29
  124.7 2.1 %fusion.10 = bf16[384,24]{0,1:T(8,128)(2,1)S(1)} fusion(bf16[3072,24]{0,1:T(8,128)(2,1)S(1)} %bitcast.69, bf16[3,3072,384]{2,1,0:T(8,128)(2,1)} %all-gather.2.cloned.1.call-done, f32[2,384,24]{1,2,0:T(8,128)S(1)} %reduce_sum.19, f32[2,384,24]{1,2,0:T(8,128)S(1)} %convert_element_type.18), kind=kOutput, calls=%fused_computation.11 | convolution fusion | flops 56650752 | bytes 2598912 | tf_op jit(solution)/shard_map/dot_general | solution.py:37
  126.8 8.7 %all_to_all.33 = bf16[8,384,24]{1,2,0:T(8,128)(2,1)S(1)} all-to-all(bf16[8,384,24]{1,2,0:T(8,128)(2,1)S(1)} %broadcast_in_dim.18), channel_id=1, replica_groups=mesh['row'=8,'z'=8,'x'=4] {'row'}, dimensions={0} | all-to-all | bytes 294912 | tf_op jit(solution)/shard_map/all_to_all | solution.py:29
  135.5 2.1 %fusion.13 = bf16[1,384,24]{1,2,0:T(8,128)(2,1)S(1)} fusion(bf16[3072,24]{0,1:T(8,128)(2,1)S(1)} %bitcast.70, bf16[3,3072,384]{2,1,0:T(8,128)(2,1)} %all-gather.2.cloned.1.call-done), kind=kOutput, calls=%fused_computation.14 | convolution fusion | flops 56632320 | bytes 2525184 | tf_op jit(solution)/shard_map/dot_general | solution.py:37
  137.6 0.1 broadcast_in_dim.19
  137.7 39.7 %all_to_all.34 = bf16[32,2,384,24]{2,3,1,0:T(8,128)(2,1)S(1)} all-to-all(bf16[32,2,384,24]{2,3,1,0:T(8,128)(2,1)S(1)} %broadcast_in_dim.19), channel_id=1, replica_groups=mesh['row'=8,'z'=8,'x'=4] {'z','x'}, dimensions={0} | all-to-all | bytes 2359296 | tf_op jit(solution)/shard_map/all_to_all | solution.py:29
  177.4 0.1 copy.39
  177.5 1.5 copy.40
  (10 shorter events, 0.2 us)
Async XLA Ops:
  6.5 62.5 %copy-start = (bf16[2,384,768]{2,1,0:T(8,128)(2,1)S(1)}, bf16[2,384,768]{2,1,0:T(8,128)(2,1)}, u32[]{:S(2)}) copy-start(bf16[2,384,768]{2,1,0:T(8,128)(2,1)} %param.7) | copy-start | bytes 3538948
  6.5 106.6 %all-gather.2.cloned.1.call-start = ((), (), s32[]{:S(2)}) async-start(), calls=%async_computation.6 | async-start | bytes 7299072 | tf_op jit(solution)/shard_map/all_gather | solution.py:46
  61.3 32.9 %all-to-all-start.1 = ((f32[8,2,384,24]{2,3,1,0:T(8,128)}), f32[8,2,384,24]{2,3,1,0:T(8,128)S(1)}, u32[]{:S(2)}, u32[]{:S(2)}) async-start(f32[8,2,384,24]{2,3,1,0:T(8,128)} %copy.35), calls=%async_computation.1 | async-start | bytes 1179648 | tf_op jit(solution)/shard_map/all_to_all | solution.py:55
Sparse Core Ops, SparseCore 0:
  9.9 103.1 all-gather.1
